TPU v7x, 128 devices: a whole 4x4x4 slice. The times are simulated.
128 devices in a mesh: section: 64 (over z, y, x), expert: 2 (over core).
Axes of the slice: x: 4, y: 4, z: 4, core: 2. Of those that a mesh axis runs over, the one named last changes fastest.
Arguments:
- state: bfloat16 [64, 2048, 3584], P('section', 'expert'), may hold values from -6 to 6
- norm_gain: float32 [64, 3584], P('section'), may hold values from 0.1 to 1.9
- router: bfloat16 [64, 3584, 128], P('section'), may hold values from -0.1875 to 0.1875
- w_gate: bfloat16 [64, 3584, 1024], P('section', None, 'expert'), may hold values from -0.09375 to 0.09375
- w_up: bfloat16 [64, 3584, 1024], P('section', None, 'expert'), may hold values from -0.09375 to 0.09375
- w_down: bfloat16 [64, 1024, 3584], P('section', 'expert'), may hold values from -0.25 to 0.25
- route_ids: int32 [1, 64, 2048, 8], P(None, 'section', 'expert'), may hold values from 0 to 127, as said below
Outputs:
- state_out: bfloat16 [64, 2048, 3584], P('section', 'expert')
Inputs may be any that keep to these rules, and one draw needn't show every extreme that they name: `route_ids`: each row names 8 different experts; expert 0 is the expert whose weights are given.
All inputs are finite; a program needn't handle non-finite values.
Results may differ from a plain program's by a relative error of at most 0.002.
Values may be sent and summed in bfloat16 or wider, within the bound.
No kernel may reach another device: no remote copies, remote signals or barrier semaphores. Data moves between devices by JAX's collectives and lax.ppermute only.
A program may use at most 128 MiB of HBM per device.

v0:
```python
import jax
import jax.numpy as jnp
from jax import lax
from jax.sharding import PartitionSpec as P

LEAD_ROWS = 256


def passed_along(x, axis, by):
    devices = lax.axis_size(axis)
    return lax.ppermute(x, axis, [(i, (i + by) % devices) for i in range(devices)])


def swapped(x, axis):
    return lax.ppermute(x, axis, [(0, 1), (1, 0)])


def expert_part(piece, gate_dev, up_dev, down_dev):
    gate = jnp.dot(piece, gate_dev, preferred_element_type=jnp.float32)
    upper = jnp.dot(piece, up_dev, preferred_element_type=jnp.float32)
    active = (jax.nn.silu(gate) * upper).astype(jnp.bfloat16)
    partial_out = jnp.dot(active, down_dev, preferred_element_type=jnp.float32)
    return lax.optimization_barrier(partial_out.astype(jnp.bfloat16))


def local(state, norm_gain, router, w_gate, w_up, w_down, route_ids):
    gate_dev = w_gate[0]
    up_dev = w_up[0]
    down_dev = w_down[0]
    gain = norm_gain[0]
    table = router[0]
    current = state[0]
    rows = current.shape[0]
    capacity = rows // 8
    bulk = rows - capacity
    chosen = jnp.sum((route_ids[0, 0] == 0).astype(jnp.int32), axis=-1)
    slot = jnp.cumsum(chosen) - chosen
    kept = (chosen > 0) & (slot < capacity)
    row_iota = jnp.arange(rows, dtype=jnp.int32)
    hole = kept & (row_iota < bulk)
    free = jnp.logical_not(kept) & (row_iota >= bulk)
    hole_rank = jnp.cumsum(hole.astype(jnp.int32)) - hole.astype(jnp.int32)
    free_rank = jnp.cumsum(free.astype(jnp.int32)) - free.astype(jnp.int32)
    n_holes = jnp.sum(hole.astype(jnp.int32))
    used = free & (free_rank < n_holes)
    top_hole, tail_used = hole[:bulk], used[bulk:]
    pairs = top_hole[:, None] & tail_used[None, :] & (hole_rank[:bulk, None] == free_rank[None, bulk:])
    tail_iota = jnp.arange(capacity, dtype=jnp.int32)
    top_mate = jnp.where(top_hole, jnp.sum(jnp.where(pairs, tail_iota[None, :], 0), axis=1), -1)
    tail_mate = jnp.where(tail_used, jnp.sum(jnp.where(pairs, row_iota[:bulk, None], 0), axis=0), -1)
    cuts = [(0, LEAD_ROWS), (LEAD_ROWS, bulk)]
    moved_first = []
    for a, b in cuts:
        fill = jnp.dot(pairs[a:b].astype(jnp.bfloat16), current[bulk:], preferred_element_type=jnp.float32)
        first = jnp.where(top_hole[a:b, None], fill.astype(jnp.bfloat16), current[a:b])
        moved_first.append(passed_along(first, "section", 1))
    me = lax.axis_index("expert")
    slot_iota = jnp.arange(capacity)[:, None]
    expert_iota = jnp.arange(table.shape[1])
    h32 = current.astype(jnp.float32)
    var = jnp.mean(h32 * h32, axis=-1, keepdims=True)
    normed = (h32 * lax.rsqrt(var + 1e-06) * gain).astype(jnp.bfloat16)
    scores = jax.nn.sigmoid(jnp.dot(normed, table, preferred_element_type=jnp.float32))
    ids = route_ids[0, 0]
    picked = jnp.sum((ids[:, :, None] == expert_iota[None, None, :]).astype(jnp.float32), axis=1)
    weight = 2.5 * scores[:, 0] * picked[:, 0] / jnp.sum(scores * picked, axis=-1)
    hit = kept[None, :] & (slot[None, :] == slot_iota)
    onehot = hit.astype(jnp.bfloat16)
    packed = jnp.dot(onehot, normed, preferred_element_type=jnp.float32).astype(jnp.bfloat16)
    other = swapped(packed, "expert")
    both = jnp.where(me == 0, jnp.concatenate([packed, other], axis=0),
                     jnp.concatenate([other, packed], axis=0))
    partials = expert_part(both, gate_dev, up_dev, down_dev)
    mine = jnp.where(me == 0, partials[:capacity], partials[capacity:])
    theirs = jnp.where(me == 0, partials[capacity:], partials[:capacity])
    summed = mine.astype(jnp.float32) + swapped(theirs, "expert").astype(jnp.float32)
    share = jnp.dot(onehot.astype(jnp.float32), weight, precision=lax.Precision.HIGHEST)
    scaled = summed * share[:, None]
    h_rows = jnp.dot(onehot, current, preferred_element_type=jnp.float32)
    new_rows = (h_rows + scaled).astype(jnp.bfloat16)
    hole_slot = jnp.sum(jnp.where(pairs, slot[:bulk, None], 0), axis=0)
    tail_slot = jnp.where(kept[bulk:], slot[bulk:], jnp.where(tail_used, hole_slot, -1))
    carry = (tail_slot[:, None] == tail_iota[None, :]).astype(jnp.bfloat16)
    carried = jnp.dot(carry, new_rows, preferred_element_type=jnp.float32).astype(jnp.bfloat16)
    second = jnp.where((tail_slot >= 0)[:, None], carried, current[bulk:])
    second = passed_along(second, "section", 1)
    mate = passed_along(jnp.concatenate([top_mate, tail_mate]), "section", 1)
    tail_mate = mate[bulk:]
    top_mate = jnp.where(row_iota < bulk, mate, -1)
    back_top = (top_mate[:, None] == tail_iota[None, :]).astype(jnp.bfloat16)
    out = jnp.where((top_mate >= 0)[:, None],
                    jnp.dot(back_top, second, preferred_element_type=jnp.float32).astype(jnp.bfloat16),
                    jnp.concatenate(moved_first + [second], axis=0))
    back_tail = (tail_mate[:, None] == row_iota[None, :bulk]).astype(jnp.bfloat16)
    low = jnp.where((tail_mate >= 0)[:, None],
                    sum(jnp.dot(back_tail[:, a:b], part, preferred_element_type=jnp.float32)
                        for (a, b), part in zip(cuts, moved_first)).astype(jnp.bfloat16),
                    second)
    out = lax.dynamic_update_slice(out, low, (bulk, 0))
    return out[None]


def solution(mesh):
    return jax.shard_map(
        local,
        mesh=mesh,
        in_specs=(
            P("section", "expert", None),
            P("section", None),
            P("section", None, None),
            P("section", None, "expert"),
            P("section", None, "expert"),
            P("section", "expert", None),
            P(None, "section", "expert", None),
        ),
        out_specs=P("section", "expert", None),
        check_vma=False,
    )
```

profile of v0, /device:TPU:1, one launch (start us, length us, event | category | flops | bytes accessed | tf_op | source)
XLA Modules:
  0.0 199.9 jit_solution(5416294582180250198)
XLA Ops:
  0.0 0.9 convert_reduce_fusion.1
  3.2 0.7 compare_and_fusion.1
  3.9 0.7 select_reduce_fusion.2
  4.7 2.1 %collective-permute-start = (s32[1024]{0:T(1024)S(1)}, s32[1024]{0:T(1024)S(1)}, u32[]{:S(2)}, u32[]{:S(2)}) collective-permute-start(s32[1024]{0:T(1024)S(1)} %pad_add_fusion), channel_id=1, source_target_pairs={{0,2},{2,4},{4,6},{6,8},{8,10},{10,12},{12,14},{14,16},{16,18},{18... | collective-permute-start | bytes 12296 | tf_op jit(solution)/shard_map/ppermute | solution.py:11
  6.8 4.6 %fusion = f32[1024]{0:T(1024)S(1)} fusion(bf16[1,1024,3584]{2,1,0:T(8,128)(2,1)} %param.7), kind=kLoop, calls=%fused_computation.2 | loop fusion | flops 11009024 | bytes 7344128 | tf_op jit(solution)/shard_map/reduce_sum | solution.py:61
  11.4 6.5 %fusion.19 = bf16[128,3584]{1,0:T(8,128)(2,1)} fusion(bf16[1,1024,3584]{2,1,0:T(8,128)(2,1)} %param.7, f32[3584]{0:T(1024)S(1)} %reduce.7, f32[1024]{0:T(1024)S(1)} %add_rsqrt_fusion, s32[1024]{0:T(1024)S(1)} %get-tuple-element.13, pred[1024]{0:T(1024)(128)(4,1)S(1)} %get-tuple-element.12), kind=kOutput, calls=%fused_computation.27 | convolution fusion | flops 954925056 | bytes 8281088 | tf_op jit(solution)/shard_map/dot_general | solution.py:69
  17.9 1.0 collective-permute-start.1
  18.9 3.7 %fusion.17 = bf16[256,3584]{1,0:T(8,128)(2,1)} fusion(bf16[1,1024,3584]{2,1,0:T(8,128)(2,1)} %param.7, pred[256]{0:T(512)(128)(4,1)S(1)} %slice.125, pred[896,128]{1,0:T(32,128)(4,1)S(1)} %get-tuple-element.10), kind=kOutput, calls=%fused_computation.23 | convolution fusion | flops 236716032 | bytes 4620800 | tf_op jit(solution)/shard_map/dot_general | solution.py:54
  22.5 1.2 collective-permute-start.4
  23.7 4.8 %fusion.16 = bf16[640,3584]{1,0:T(8,128)(2,1)} fusion(bf16[1,1024,3584]{2,1,0:T(8,128)(2,1)} %param.7, pred[640]{0:T(1024)(128)(4,1)S(1)} %slice.129, pred[896,128]{1,0:T(32,128)(4,1)S(1)} %get-tuple-element.10), kind=kOutput, calls=%fused_computation.20 | convolution fusion | flops 591790080 | bytes 10175488 | tf_op jit(solution)/shard_map/dot_general | solution.py:54
  28.5 0.9 collective-permute-start.5
  29.7 5.7 %convert_reduce_fusion = f32[1024,128]{1,0:T(8,128)S(1)} fusion(s32[1024,8]{1,0:T(8,128)S(1)} %copy.10), kind=kLoop, calls=%fused_computation.29 | loop fusion | flops 3014656 | bytes 557056 | tf_op jit(solution)/shard_map/reduce_sum | solution.py:65
  35.6 5.2 %fusion.26 = f32[256,512]{1,0:T(8,128)} fusion(bf16[1,3584,512]{2,1,0:T(8,128)(2,1)} %param.10, bf16[128,3584]{1,0:T(8,128)(2,1)} %collective-permute-done.1, bf16[128,3584]{1,0:T(8,128)(2,1)} %fusion.19, pred[]{:T(512)S(6)} %eq.103), kind=kOutput, calls=%fused_computation.34 | convolution fusion | flops 947781632 | bytes 6029313 | tf_op jit(solution)/shard_map/dot_general | solution.py:19
  40.9 6.6 %convolution_convert_fusion.3 = bf16[256,3584]{1,0:T(8,128)(2,1)S(1)} fusion(bf16[1,512,3584]{2,1,0:T(8,128)(2,1)} %param.12, f32[256,512]{1,0:T(8,128)} %fusion.26, bf16[1,3584,512]{2,1,0:T(8,128)(2,1)} %param.11, bf16[128,3584]{1,0:T(8,128)(2,1)} %collective-permute-done.1, bf16[128,3584]{1,0:T(8,128)(2,1)} %fusion.19, pred[]{:T(512)S(6)} %eq.103), kind=kOutput, calls=%fused_computation.22 | convolution fusion | flops 1889009664 | bytes 11534337 | tf_op jit(solution)/shard_map/dot_general | solution.py:22
  47.5 0.8 collective-permute-start.2
  48.3 5.3 %multiply_reduce_fusion = (f32[1024]{0:T(1024)S(1)}, f32[1024,128]{0,1:T(8,128)S(1)}) fusion(f32[1024,128]{0,1:T(8,128)S(1)} %copy.11, bf16[1,3584,128]{2,1,0:T(8,128)(2,1)S(1)} %copy-done, bf16[1,1024,3584]{2,1,0:T(8,128)(2,1)} %param.7, f32[3584]{0:T(1024)S(1)} %reduce.7, f32[1024]{0:T(1024)S(1)} %add_rsqrt_fusion), kind=kOutput, calls=%fused_computation.55 | convolution fusion | flops 954858496 | bytes 9328640 | tf_op jit(solution)/shard_map/dot_general | solution.py:63
  54.1 0.9 copy-done.3
  55.0 6.3 %fusion.22 = bf16[128,3584]{1,0:T(8,128)(2,1)} fusion(bf16[128,3584]{1,0:T(8,128)(2,1)} %copy-done.3, f32[128]{0:T(128)S(1)} %convolution_bitcast_fusion, pred[128]{0:T(512)(128)(4,1)S(1)} %get-tuple-element.8, pred[]{:T(512)S(6)} %eq.103, bf16[1,1024,3584]{2,1,0:T(8,128)(2,1)} %param.7, bf16[256,3584]{1,0:T(8,128)(2,1)S(1)} %convolution_convert_fusion.3, ...), kind=kOutput, calls=%fused_computation.28 | convolution fusion | flops 1061371904 | bytes 11933825 | tf_op jit(solution)/shard_map/dot_general | solution.py:84
  61.3 1.2 collective-permute-start.3
  62.7 105.5 %collective-permute-done.5 = bf16[640,3584]{1,0:T(8,128)(2,1)} collective-permute-done((bf16[640,3584]{1,0:T(8,128)(2,1)}, bf16[640,3584]{1,0:T(8,128)(2,1)}, u32[]{:S(2)}, u32[]{:S(2)}) %collective-permute-start.5) | collective-permute-done | bytes 4587552 | tf_op jit(solution)/shard_map/ppermute | solution.py:11
  168.2 3.2 %fusion.59 = f32[128,3584]{1,0:T(8,128)S(1)} fusion(bf16[640,3584]{1,0:T(8,128)(2,1)} %collective-permute-done.5, pred[128,896]{1,0:T(32,128)(4,1)S(1)} %broadcast_compare_fusion), kind=kOutput, calls=%fused_computation.64 | convolution fusion | flops 587202560 | bytes 6504448 | tf_op jit(solution)/shard_map/dot_general | solution.py:96
  171.4 16.3 %collective-permute-done.3 = bf16[128,3584]{1,0:T(8,128)(2,1)S(1)} collective-permute-done((bf16[128,3584]{1,0:T(8,128)(2,1)}, bf16[128,3584]{1,0:T(8,128)(2,1)S(1)}, u32[]{:S(2)}, u32[]{:S(2)}) %collective-permute-start.3) | collective-permute-done | bytes 917536 | tf_op jit(solution)/shard_map/ppermute | solution.py:11
  187.8 9.2 %fusion.8 = bf16[1,1024,3584]{2,1,0:T(8,128)(2,1)} fusion(bf16[128,3584]{1,0:T(8,128)(2,1)S(1)} %collective-permute-done.3, bf16[640,3584]{1,0:T(8,128)(2,1)} %collective-permute-done.5, bf16[256,3584]{1,0:T(8,128)(2,1)} %collective-permute-done.4, pred[1024]{0:T(1024)(128)(4,1)S(1)} %broadcast_compare_fusion.1, s32[1024]{0:T(1024)S(1)} %fusion.83), kind=kOutput, calls=%fused_computation.11 | convolution fusion | flops 969015296 | bytes 14685184 | tf_op jit(solution)/shard_map/dot_general | solution.py:92
  197.0 2.9 %bitcast_dynamic-update-slice_fusion = bf16[1,1024,3584]{2,1,0:T(8,128)(2,1)} fusion(bf16[1,1024,3584]{2,1,0:T(8,128)(2,1)} %fusion.8, bf16[128,3584]{1,0:T(8,128)(2,1)S(1)} %collective-permute-done.3, pred[128]{0:T(512)(128)(4,1)S(1)} %broadcast_compare_fusion.2, f32[128,3584]{1,0:T(8,128)S(1)} %fusion.59, bf16[256,3584]{1,0:T(8,128)(2,1)} %collective-permute-done.4, ...), kind=kOutput, calls=%fused_computation.43 | convolution fusion | flops 236257280 | bytes 5538304 | tf_op jit(solution)/shard_map/dot_general | solution.py:96
  (49 shorter events, 3.4 us)
Async XLA Ops:
  0.0 48.3 %copy-start = (bf16[1,3584,128]{2,1,0:T(8,128)(2,1)S(1)}, bf16[1,3584,128]{2,1,0:T(8,128)(2,1)}, u32[]{:S(2)}) copy-start(bf16[1,3584,128]{2,1,0:T(8,128)(2,1)} %param.9) | copy-start | bytes 2752516
  4.6 6.7 %copy-start.2 = (f32[1,3584]{1,0:T(1,128)S(1)}, f32[1,3584]{1,0:T(1,128)}, u32[]{:S(2)}) copy-start(f32[1,3584]{1,0:T(1,128)} %param.8) | copy-start | bytes 43012
  4.7 49.4 %collective-permute-start = (s32[1024]{0:T(1024)S(1)}, s32[1024]{0:T(1024)S(1)}, u32[]{:S(2)}, u32[]{:S(2)}) collective-permute-start(s32[1024]{0:T(1024)S(1)} %pad_add_fusion), channel_id=1, source_target_pairs={{0,2},{2,4},{4,6},{6,8},{8,10},{10,12},{12,14},{14,16},{16,18},{18... | collective-permute-start | bytes 12296 | tf_op jit(solution)/shard_map/ppermute | solution.py:11
  17.9 17.7 %collective-permute-start.1 = (bf16[128,3584]{1,0:T(8,128)(2,1)}, bf16[128,3584]{1,0:T(8,128)(2,1)}, u32[]{:S(2)}, u32[]{:S(2)}) collective-permute-start(bf16[128,3584]{1,0:T(8,128)(2,1)} %fusion.19), channel_id=1, source_target_pairs={{0,1},{1,0},{2,3},{3,2},{4,5},{5,4},{6,7},{7,6},{8,9},{9,8},{10,11... | collective-permute-start | bytes 2752520 | tf_op jit(solution)/shard_map/ppermute | solution.py:15
  22.5 148.9 %collective-permute-start.4 = (bf16[256,3584]{1,0:T(8,128)(2,1)}, bf16[256,3584]{1,0:T(8,128)(2,1)}, u32[]{:S(2)}, u32[]{:S(2)}) collective-permute-start(bf16[256,3584]{1,0:T(8,128)(2,1)} %fusion.17), channel_id=1, source_target_pairs={{0,2},{2,4},{4,6},{6,8},{8,10},{10,12},{12,14},{14,16},{16,18},{18... | collective-permute-start | bytes 5505032 | tf_op jit(solution)/shard_map/ppermute | solution.py:11
  23.7 5.7 %copy-start.1 = (s32[1,1,1024,8]{2,3,1,0:T(8,128)S(1)}, s32[1,1,1024,8]{2,3,1,0:T(8,128)}, u32[]{:S(2)}) copy-start(s32[1,1,1024,8]{2,3,1,0:T(8,128)} %param.13) | copy-start | bytes 98308
  28.5 139.7 %collective-permute-start.5 = (bf16[640,3584]{1,0:T(8,128)(2,1)}, bf16[640,3584]{1,0:T(8,128)(2,1)}, u32[]{:S(2)}, u32[]{:S(2)}) collective-permute-start(bf16[640,3584]{1,0:T(8,128)(2,1)} %fusion.16), channel_id=1, source_target_pairs={{0,2},{2,4},{4,6},{6,8},{8,10},{10,12},{12,14},{14,16},{16,18},{18... | collective-permute-start | bytes 13762568 | tf_op jit(solution)/shard_map/ppermute | solution.py:11
  47.5 6.6 %collective-permute-start.2 = (bf16[128,3584]{1,0:T(8,128)(2,1)S(1)}, bf16[128,3584]{1,0:T(8,128)(2,1)S(1)}, u32[]{:S(2)}, u32[]{:S(2)}) collective-permute-start(bf16[128,3584]{1,0:T(8,128)(2,1)S(1)} %broadcast_select_fusion), channel_id=1, source_target_pairs={{0,1},{1,0},{2,3},{3,2},{4,5},{5,4},{6,7},{7,6},{8,9},{9,8},{10,11... | collective-permute-start | bytes 2752520 | tf_op jit(solution)/shard_map/ppermute | solution.py:15
  54.1 0.9 copy-start.3
  61.3 126.4 %collective-permute-start.3 = (bf16[128,3584]{1,0:T(8,128)(2,1)}, bf16[128,3584]{1,0:T(8,128)(2,1)S(1)}, u32[]{:S(2)}, u32[]{:S(2)}) collective-permute-start(bf16[128,3584]{1,0:T(8,128)(2,1)} %fusion.22), channel_id=1, source_target_pairs={{0,2},{2,4},{4,6},{6,8},{8,10},{10,12},{12,14},{14,16},{16,18},{18... | collective-permute-start | bytes 2752520 | tf_op jit(solution)/shard_map/ppermute | solution.py:11
where the time goes:
time: 200 us
  waiting for transfers between devices  122 us (61%)
  matrix products  54 us (27%)
  other arithmetic  14.7 us (7%)
  starting transfers between devices  7.2 us (4%)
    ppermute x4, waiting for transfers between devices, passed_along(): lax.ppermute(x, axis, [(i, (i + by) % devices) for i in range(devices)])  122 us
    dot_general x1, matrix products, local(): jnp.dot(back_top, second, preferred_element_type=jnp.float32)  9.23 us
    dot_general x2, matrix products, local(): jnp.dot(pairs[a:b].astype(jnp.bfloat16), current[bulk:], preferred_elemen...  8.47 us
    dot_general x1, matrix products, expert_part(): partial_out = jnp.dot(active, down_dev, preferred_element_type=jnp.float32)  6.55 us
    dot_general x1, matrix products, local(): jnp.dot(onehot, normed, preferred_element_type=jnp.float32)  6.5 us
    dot_general x1, matrix products, local(): jnp.dot(carry, new_rows, preferred_element_type=jnp.float32)  6.3 us
    dot_general x2, matrix products, local(): jnp.dot(back_tail[:, a:b], part, preferred_element_type=jnp.float32)  6.11 us
    reduce_sum x1, other arithmetic, local(): jnp.sum((ids[:, :, None] == expert_iota[None, None, :]).astype(jnp.float3...  5.75 us
  transfers between devices with their start and end apart: 6, of which 2 were waited for; matrix products, arithmetic and copies ran while one was open for 27% of the time, Pallas kernels for 0%

commit v1 on v0

--- a/solution.py
+++ b/solution.py
@@ -3,7 +3,7 @@
 from jax import lax
 from jax.sharding import PartitionSpec as P
 
-LEAD_ROWS = 256
+LEAD_ROWS = 64
 
 
 def passed_along(x, axis, by):
@@ -83,8 +83,9 @@
     carry = (tail_slot[:, None] == tail_iota[None, :]).astype(jnp.bfloat16)
     carried = jnp.dot(carry, new_rows, preferred_element_type=jnp.float32).astype(jnp.bfloat16)
     second = jnp.where((tail_slot >= 0)[:, None], carried, current[bulk:])
+    second, mate = lax.optimization_barrier((second, jnp.concatenate([top_mate, tail_mate])))
     second = passed_along(second, "section", 1)
-    mate = passed_along(jnp.concatenate([top_mate, tail_mate]), "section", 1)
+    mate = passed_along(mate, "section", 1)
     tail_mate = mate[bulk:]
     top_mate = jnp.where(row_iota < bulk, mate, -1)
     back_top = (top_mate[:, None] == tail_iota[None, :]).astype(jnp.bfloat16)

time: 200 us -> 200 us (level)
  matrix products: 54 us -> 50.9 us
  waiting for transfers between devices: 122 us -> 125 us
  transfers between devices with their start and end apart: 6 -> 6, of which waited for: 2 -> 4; matrix products, arithmetic and copies ran while one was open for 27% -> 23% of each run, Pallas kernels for 0% -> 0%
where the time goes in v1:
time: 200 us
  waiting for transfers between devices  125 us (62%)
  matrix products  50.9 us (25%)
  other arithmetic  15.4 us (8%)
  starting transfers between devices  6.48 us (3%)
  local copies, waits for them, and re-layouts  2.02 us (1%)
    ppermute x4, waiting for transfers between devices, passed_along(): lax.ppermute(x, axis, [(i, (i + by) % devices) for i in range(devices)])  124 us
    dot_general x1, matrix products, local(): jnp.dot(back_top, second, preferred_element_type=jnp.float32)  8.56 us
    dot_general x2, matrix products, local(): jnp.dot(pairs[a:b].astype(jnp.bfloat16), current[bulk:], preferred_elemen...  7.19 us
    dot_general x1, matrix products, local(): jnp.dot(normed, table, preferred_element_type=jnp.float32)  6.54 us
    dot_general x1, matrix products, expert_part(): partial_out = jnp.dot(active, down_dev, preferred_element_type=jnp.float32)  6.53 us
    dot_general x1, matrix products, local(): jnp.dot(onehot, normed, preferred_element_type=jnp.float32)  6.45 us
    dot_general x1, matrix products, local(): jnp.dot(carry, new_rows, preferred_element_type=jnp.float32)  6.06 us
    reduce_sum x1, other arithmetic, local(): jnp.sum((ids[:, :, None] == expert_iota[None, None, :]).astype(jnp.float3...  5.75 us
  transfers between devices with their start and end apart: 6, of which 4 were waited for; matrix products, arithmetic and copies ran while one was open for 23% of the time, Pallas kernels for 0%

profile of v1, /device:TPU:1, one launch (start us, length us, event | category | flops | bytes accessed | tf_op | source)
XLA Modules:
  0.0 199.9 jit_solution(6481403209455038302)
XLA Ops:
  0.0 0.9 convert_reduce_fusion.1
  1.4 4.6 %fusion = f32[1024]{0:T(1024)S(1)} fusion(bf16[1,1024,3584]{2,1,0:T(8,128)(2,1)} %param.7), kind=kLoop, calls=%fused_computation.2 | loop fusion | flops 11009024 | bytes 7344128 | tf_op jit(solution)/shard_map/reduce_sum | solution.py:61
  6.1 6.5 %fusion.17 = bf16[128,3584]{1,0:T(8,128)(2,1)} fusion(bf16[1,1024,3584]{2,1,0:T(8,128)(2,1)} %param.7, f32[3584]{0:T(1024)S(1)} %reduce.7, f32[1024]{0:T(1024)S(1)} %add_rsqrt_fusion, s32[1024]{0:T(1024)S(1)} %get-tuple-element.17, pred[1024]{0:T(1024)(128)(4,1)S(1)} %get-tuple-element.16), kind=kOutput, calls=%fused_computation.25 | convolution fusion | flops 954925056 | bytes 8281088 | tf_op jit(solution)/shard_map/dot_general | solution.py:69
  12.5 1.4 collective-permute-start
  17.2 5.6 %bitcast_select_fusion = bf16[832,3584]{1,0:T(8,128)(2,1)} fusion(bf16[1,1024,3584]{2,1,0:T(8,128)(2,1)} %param.7, pred[832]{0:T(1024)(128)(4,1)S(1)} %slice.129, pred[896,128]{1,0:T(32,128)(4,1)S(1)} %get-tuple-element.14), kind=kOutput, calls=%fused_computation.20 | convolution fusion | flops 769327104 | bytes 12952576 | tf_op jit(solution)/shard_map/dot_general | solution.py:54
  22.8 1.3 collective-permute-start.5
  24.3 5.7 %convert_reduce_fusion = f32[1024,128]{1,0:T(8,128)S(1)} fusion(s32[1024,8]{1,0:T(8,128)S(1)} %copy.10), kind=kLoop, calls=%fused_computation.29 | loop fusion | flops 3014656 | bytes 557056 | tf_op jit(solution)/shard_map/reduce_sum | solution.py:65
  30.3 6.5 %multiply_reduce_fusion = (f32[1024]{0:T(1024)S(1)}, f32[1024,128]{0,1:T(8,128)}) fusion(f32[1024,128]{0,1:T(8,128)S(1)} %copy.11, bf16[1,3584,128]{2,1,0:T(8,128)(2,1)S(1)} %copy-done, bf16[1,1024,3584]{2,1,0:T(8,128)(2,1)} %param.7, f32[3584]{0:T(1024)S(1)} %reduce.7, f32[1024]{0:T(1024)S(1)} %add_rsqrt_fusion), kind=kOutput, calls=%fused_computation.56 | convolution fusion | flops 954858496 | bytes 9328640 | tf_op jit(solution)/shard_map/dot_general | solution.py:63
  36.9 4.1 %fusion.25 = f32[256,512]{1,0:T(8,128)} fusion(bf16[1,3584,512]{2,1,0:T(8,128)(2,1)S(1)} %copy-done.3, bf16[128,3584]{1,0:T(8,128)(2,1)} %collective-permute-done, bf16[128,3584]{1,0:T(8,128)(2,1)} %fusion.17, pred[]{:T(512)S(6)} %eq.100), kind=kOutput, calls=%fused_computation.34 | convolution fusion | flops 947781632 | bytes 6029313 | tf_op jit(solution)/shard_map/dot_general | solution.py:19
  40.9 6.5 %convolution_convert_fusion.2 = bf16[256,3584]{1,0:T(8,128)(2,1)S(1)} fusion(bf16[1,512,3584]{2,1,0:T(8,128)(2,1)} %param.12, f32[256,512]{1,0:T(8,128)} %fusion.25, bf16[1,3584,512]{2,1,0:T(8,128)(2,1)} %param.11, bf16[128,3584]{1,0:T(8,128)(2,1)} %collective-permute-done, bf16[128,3584]{1,0:T(8,128)(2,1)} %fusion.17, pred[]{:T(512)S(6)} %eq.100), kind=kOutput, calls=%fused_computation.21 | convolution fusion | flops 1889009664 | bytes 11534337 | tf_op jit(solution)/shard_map/dot_general | solution.py:22
  47.9 0.8 slice_multiply_fusion
  49.1 1.0 collective-permute-done.1
  50.1 0.9 copy-done.4
  51.1 6.1 %fusion.20 = bf16[128,3584]{1,0:T(8,128)(2,1)} fusion(bf16[128,3584]{1,0:T(8,128)(2,1)} %copy-done.4, f32[128]{0:T(128)S(1)} %convolution_bitcast_fusion, pred[128]{0:T(512)(128)(4,1)S(1)} %get-tuple-element.12, pred[]{:T(512)S(6)} %eq.100, bf16[1,1024,3584]{2,1,0:T(8,128)(2,1)} %param.7, bf16[256,3584]{1,0:T(8,128)(2,1)S(1)} %convolution_convert_fusion.2, ...), kind=kOutput, calls=%fused_computation.26 | convolution fusion | flops 1061371904 | bytes 11933825 | tf_op jit(solution)/shard_map/dot_general | solution.py:84
  57.1 1.2 collective-permute-start.2
  58.3 1.6 fusion.21
  59.9 1.0 collective-permute-start.4
  60.9 1.2 collective-permute-start.3
  62.1 98.5 %collective-permute-done.2 = s32[1024]{0:T(1024)S(1)} collective-permute-done((s32[1024]{0:T(1024)S(1)}, s32[1024]{0:T(1024)S(1)}, u32[]{:S(2)}, u32[]{:S(2)}) %collective-permute-start.2) | collective-permute-done | bytes 4128 | tf_op jit(solution)/shard_map/ppermute | solution.py:11
  160.8 3.9 %fusion.58 = f32[128,3584]{1,0:T(8,128)S(1)} fusion(bf16[832,3584]{1,0:T(8,128)(2,1)} %collective-permute-done.5, pred[128,896]{1,0:T(32,128)(4,1)S(1)} %broadcast_compare_fusion), kind=kOutput, calls=%fused_computation.63 | convolution fusion | flops 763363328 | bytes 7913472 | tf_op jit(solution)/shard_map/dot_general | solution.py:97
  164.7 5.6 %collective-permute-done.4 = bf16[64,3584]{1,0:T(8,128)(2,1)S(1)} collective-permute-done((bf16[64,3584]{1,0:T(8,128)(2,1)S(1)}, bf16[64,3584]{1,0:T(8,128)(2,1)S(1)}, u32[]{:S(2)}, u32[]{:S(2)}) %collective-permute-start.4) | collective-permute-done | bytes 458784 | tf_op jit(solution)/shard_map/ppermute | solution.py:11
  170.3 19.7 %collective-permute-done.3 = bf16[128,3584]{1,0:T(8,128)(2,1)S(1)} collective-permute-done((bf16[128,3584]{1,0:T(8,128)(2,1)}, bf16[128,3584]{1,0:T(8,128)(2,1)S(1)}, u32[]{:S(2)}, u32[]{:S(2)}) %collective-permute-start.3) | collective-permute-done | bytes 917536 | tf_op jit(solution)/shard_map/ppermute | solution.py:11
  190.0 8.6 %fusion.8 = bf16[1,1024,3584]{2,1,0:T(8,128)(2,1)} fusion(bf16[128,3584]{1,0:T(8,128)(2,1)S(1)} %collective-permute-done.3, bf16[832,3584]{1,0:T(8,128)(2,1)} %collective-permute-done.5, bf16[64,3584]{1,0:T(8,128)(2,1)S(1)} %collective-permute-done.4, pred[1024]{0:T(1024)(128)(4,1)S(1)} %broadcast_compare_fusion.1, s32[1024]{0:T(1024)S(1)} %fusion.82), kind=kOutput, calls=%fused_computation.11 | convolution fusion | flops 969015296 | bytes 14685184 | tf_op jit(solution)/shard_map/dot_general | solution.py:93
  198.5 1.3 bitcast_dynamic-update-slice_fusion
  (51 shorter events, 5.3 us)
Async XLA Ops:
  0.0 30.3 %copy-start = (bf16[1,3584,128]{2,1,0:T(8,128)(2,1)S(1)}, bf16[1,3584,128]{2,1,0:T(8,128)(2,1)}, u32[]{:S(2)}) copy-start(bf16[1,3584,128]{2,1,0:T(8,128)(2,1)} %param.9) | copy-start | bytes 2752516
  1.4 4.7 %copy-start.2 = (f32[1,3584]{1,0:T(1,128)S(1)}, f32[1,3584]{1,0:T(1,128)}, u32[]{:S(2)}) copy-start(f32[1,3584]{1,0:T(1,128)} %param.8) | copy-start | bytes 43012
  12.5 24.3 %collective-permute-start = (bf16[128,3584]{1,0:T(8,128)(2,1)}, bf16[128,3584]{1,0:T(8,128)(2,1)}, u32[]{:S(2)}, u32[]{:S(2)}) collective-permute-start(bf16[128,3584]{1,0:T(8,128)(2,1)} %fusion.17), channel_id=1, source_target_pairs={{0,1},{1,0},{2,3},{3,2},{4,5},{5,4},{6,7},{7,6},{8,9},{9,8},{10,11... | collective-permute-start | bytes 2752520 | tf_op jit(solution)/shard_map/ppermute | solution.py:15
  17.2 7.0 %copy-start.1 = (s32[1,1,1024,8]{2,3,1,0:T(8,128)S(1)}, s32[1,1,1024,8]{2,3,1,0:T(8,128)}, u32[]{:S(2)}) copy-start(s32[1,1,1024,8]{2,3,1,0:T(8,128)} %param.13) | copy-start | bytes 98308
  22.8 138.0 %collective-permute-start.5 = (bf16[832,3584]{1,0:T(8,128)(2,1)}, bf16[832,3584]{1,0:T(8,128)(2,1)}, u32[]{:S(2)}, u32[]{:S(2)}) collective-permute-start(bf16[832,3584]{1,0:T(8,128)(2,1)} %bitcast_select_fusion), channel_id=1, source_target_pairs={{0,2},{2,4},{4,6},{6,8},{8,10},{10,12},{12,14},{14,16},{16,18},{18... | collective-permute-start | bytes 17891336 | tf_op jit(solution)/shard_map/ppermute | solution.py:11
  30.3 6.6 %copy-start.3 = (bf16[1,3584,512]{2,1,0:T(8,128)(2,1)S(1)}, bf16[1,3584,512]{2,1,0:T(8,128)(2,1)}, u32[]{:S(2)}) copy-start(bf16[1,3584,512]{2,1,0:T(8,128)(2,1)} %param.10) | copy-start | bytes 11010052
  47.6 2.6 %collective-permute-start.1 = (bf16[128,3584]{1,0:T(8,128)(2,1)S(1)}, bf16[128,3584]{1,0:T(8,128)(2,1)S(1)}, u32[]{:S(2)}, u32[]{:S(2)}) collective-permute-start(bf16[128,3584]{1,0:T(8,128)(2,1)S(1)} %broadcast_select_fusion), channel_id=1, source_target_pairs={{0,1},{1,0},{2,3},{3,2},{4,5},{5,4},{6,7},{7,6},{8,9},{9,8},{10,11... | collective-permute-start | bytes 2752520 | tf_op jit(solution)/shard_map/ppermute | solution.py:15
  50.1 0.9 copy-start.4
  57.1 103.5 %collective-permute-start.2 = (s32[1024]{0:T(1024)S(1)}, s32[1024]{0:T(1024)S(1)}, u32[]{:S(2)}, u32[]{:S(2)}) collective-permute-start(s32[1024]{0:T(1024)S(1)} %pad_add_fusion), channel_id=1, source_target_pairs={{0,2},{2,4},{4,6},{6,8},{8,10},{10,12},{12,14},{14,16},{16,18},{18... | collective-permute-start | bytes 12296 | tf_op jit(solution)/shard_map/ppermute | solution.py:11
  59.9 110.4 %collective-permute-start.4 = (bf16[64,3584]{1,0:T(8,128)(2,1)S(1)}, bf16[64,3584]{1,0:T(8,128)(2,1)S(1)}, u32[]{:S(2)}, u32[]{:S(2)}) collective-permute-start(bf16[64,3584]{1,0:T(8,128)(2,1)S(1)} %fusion.21), channel_id=1, source_target_pairs={{0,2},{2,4},{4,6},{6,8},{8,10},{10,12},{12,14},{14,16},{16,18},{18... | collective-permute-start | bytes 1376264 | tf_op jit(solution)/shard_map/ppermute | solution.py:11
  60.9 129.1 %collective-permute-start.3 = (bf16[128,3584]{1,0:T(8,128)(2,1)}, bf16[128,3584]{1,0:T(8,128)(2,1)S(1)}, u32[]{:S(2)}, u32[]{:S(2)}) collective-permute-start(bf16[128,3584]{1,0:T(8,128)(2,1)} %fusion.20), channel_id=1, source_target_pairs={{0,2},{2,4},{4,6},{6,8},{8,10},{10,12},{12,14},{14,16},{16,18},{18... | collective-permute-start | bytes 2752520 | tf_op jit(solution)/shard_map/ppermute | solution.py:11

commit v2 on v1

--- a/solution.py
+++ b/solution.py
@@ -34,13 +34,19 @@
     capacity = rows // 8
     bulk = rows - capacity
     chosen = jnp.sum((route_ids[0, 0] == 0).astype(jnp.int32), axis=-1)
-    slot = jnp.cumsum(chosen) - chosen
+    row_iota = jnp.arange(rows, dtype=jnp.int32)
+    before = (row_iota[None, :] < row_iota[:, None]).astype(jnp.bfloat16)
+
+    def earlier(*cols):
+        stack = jnp.stack(cols, axis=1).astype(jnp.bfloat16)
+        sums = jnp.dot(before, stack, preferred_element_type=jnp.float32).astype(jnp.int32)
+        return [sums[:, k] for k in range(len(cols))]
+
+    (slot,) = earlier(chosen)
     kept = (chosen > 0) & (slot < capacity)
-    row_iota = jnp.arange(rows, dtype=jnp.int32)
     hole = kept & (row_iota < bulk)
     free = jnp.logical_not(kept) & (row_iota >= bulk)
-    hole_rank = jnp.cumsum(hole.astype(jnp.int32)) - hole.astype(jnp.int32)
-    free_rank = jnp.cumsum(free.astype(jnp.int32)) - free.astype(jnp.int32)
+    hole_rank, free_rank = earlier(hole, free)
     n_holes = jnp.sum(hole.astype(jnp.int32))
     used = free & (free_rank < n_holes)
     top_hole, tail_used = hole[:bulk], used[bulk:]

time: 200 us -> 200 us (level)
  transfers between devices with their start and end apart: 6 -> 6, of which waited for: 4 -> 4; matrix products, arithmetic and copies ran while one was open for 23% -> 22% of each run, Pallas kernels for 0% -> 0%
where the time goes in v2:
time: 200 us; the launch traced here: 199 us
  waiting for transfers between devices  125 us (62%)
  matrix products  52 us (26%)
  other arithmetic  14.3 us (7%)
  starting transfers between devices  6.49 us (3%)
    ppermute x4, waiting for transfers between devices, passed_along(): lax.ppermute(x, axis, [(i, (i + by) % devices) for i in range(devices)])  124 us
    dot_general x1, matrix products, local(): jnp.dot(back_top, second, preferred_element_type=jnp.float32)  8.65 us
    dot_general x2, matrix products, local(): jnp.dot(pairs[a:b].astype(jnp.bfloat16), current[bulk:], preferred_elemen...  7.18 us
    dot_general x1, matrix products, local(): jnp.dot(normed, table, preferred_element_type=jnp.float32)  6.55 us
    dot_general x1, matrix products, expert_part(): partial_out = jnp.dot(active, down_dev, preferred_element_type=jnp.float32)  6.52 us
    dot_general x1, matrix products, local(): jnp.dot(onehot, normed, preferred_element_type=jnp.float32)  6.46 us
    dot_general x1, matrix products, local(): jnp.dot(carry, new_rows, preferred_element_type=jnp.float32)  6.1 us
    reduce_sum x1, other arithmetic, local(): jnp.sum((ids[:, :, None] == expert_iota[None, None, :]).astype(jnp.float3...  5.75 us
  transfers between devices with their start and end apart: 6, of which 4 were waited for; matrix products, arithmetic and copies ran while one was open for 22% of the time, Pallas kernels for 0%

profile of v2, /device:TPU:1, one launch (start us, length us, event | category | flops | bytes accessed | tf_op | source)
XLA Modules:
  0.0 199.3 jit_solution(8125916096939909598)
XLA Ops:
  0.0 0.9 convert_reduce_fusion.1
  2.0 4.6 %fusion = f32[1024]{0:T(1024)S(1)} fusion(bf16[1,1024,3584]{2,1,0:T(8,128)(2,1)} %param.7), kind=kLoop, calls=%fused_computation.2 | loop fusion | flops 11009024 | bytes 7344128 | tf_op jit(solution)/shard_map/reduce_sum | solution.py:67
  6.7 6.5 %fusion.17 = bf16[128,3584]{1,0:T(8,128)(2,1)} fusion(bf16[1,1024,3584]{2,1,0:T(8,128)(2,1)} %param.7, f32[3584]{0:T(1024)S(1)} %reduce.2, f32[1024]{0:T(1024)S(1)} %add_rsqrt_fusion, s32[1024]{0:T(1024)S(1)} %convert_element_type.80, pred[1024]{0:T(1024)(128)(4,1)S(1)} %get-tuple-element.16), kind=kOutput, calls=%fused_computation.25 | convolution fusion | flops 954925056 | bytes 8281088 | tf_op jit(solution)/shard_map/dot_general | solution.py:75
  13.1 1.4 collective-permute-start
  16.5 5.6 %bitcast_select_fusion = bf16[832,3584]{1,0:T(8,128)(2,1)} fusion(bf16[1,1024,3584]{2,1,0:T(8,128)(2,1)} %param.7, pred[832]{0:T(1024)(128)(4,1)S(1)} %slice.115, pred[896,128]{1,0:T(32,128)(4,1)S(1)} %get-tuple-element.14), kind=kOutput, calls=%fused_computation.20 | convolution fusion | flops 769327104 | bytes 12952576 | tf_op jit(solution)/shard_map/dot_general | solution.py:60
  22.1 1.3 collective-permute-start.5
  23.7 5.7 %convert_reduce_fusion = f32[1024,128]{1,0:T(8,128)S(1)} fusion(s32[1024,8]{1,0:T(8,128)S(1)} %copy.10), kind=kLoop, calls=%fused_computation.29 | loop fusion | flops 3014656 | bytes 557056 | tf_op jit(solution)/shard_map/reduce_sum | solution.py:71
  29.6 6.5 %multiply_reduce_fusion = (f32[1024]{0:T(1024)S(1)}, f32[1024,128]{0,1:T(8,128)}) fusion(f32[1024,128]{0,1:T(8,128)S(1)} %copy.11, bf16[1,3584,128]{2,1,0:T(8,128)(2,1)S(1)} %copy-done, bf16[1,1024,3584]{2,1,0:T(8,128)(2,1)} %param.7, f32[3584]{0:T(1024)S(1)} %reduce.2, f32[1024]{0:T(1024)S(1)} %add_rsqrt_fusion), kind=kOutput, calls=%fused_computation.60 | convolution fusion | flops 954858496 | bytes 9328640 | tf_op jit(solution)/shard_map/dot_general | solution.py:69
  36.2 4.0 %fusion.27 = f32[256,512]{1,0:T(8,128)} fusion(bf16[1,3584,512]{2,1,0:T(8,128)(2,1)S(1)} %copy-done.3, bf16[128,3584]{1,0:T(8,128)(2,1)} %collective-permute-done, bf16[128,3584]{1,0:T(8,128)(2,1)} %fusion.17, pred[]{:T(512)S(6)} %eq.106), kind=kOutput, calls=%fused_computation.37 | convolution fusion | flops 947781632 | bytes 6029313 | tf_op jit(solution)/shard_map/dot_general | solution.py:19
  40.2 6.5 %convolution_convert_fusion.2 = bf16[256,3584]{1,0:T(8,128)(2,1)S(1)} fusion(bf16[1,512,3584]{2,1,0:T(8,128)(2,1)} %param.12, f32[256,512]{1,0:T(8,128)} %fusion.27, bf16[1,3584,512]{2,1,0:T(8,128)(2,1)} %param.11, bf16[128,3584]{1,0:T(8,128)(2,1)} %collective-permute-done, bf16[128,3584]{1,0:T(8,128)(2,1)} %fusion.17, pred[]{:T(512)S(6)} %eq.106), kind=kOutput, calls=%fused_computation.21 | convolution fusion | flops 1889009664 | bytes 11534337 | tf_op jit(solution)/shard_map/dot_general | solution.py:22
  47.2 0.8 slice_multiply_fusion
  48.4 1.0 collective-permute-done.1
  49.4 0.9 copy-done.4
  50.3 6.1 %fusion.20 = bf16[128,3584]{1,0:T(8,128)(2,1)} fusion(bf16[128,3584]{1,0:T(8,128)(2,1)} %copy-done.4, f32[128]{0:T(128)S(1)} %convolution_bitcast_fusion, pred[128]{0:T(512)(128)(4,1)S(1)} %get-tuple-element.12, pred[]{:T(512)S(6)} %eq.106, bf16[1,1024,3584]{2,1,0:T(8,128)(2,1)} %param.7, bf16[256,3584]{1,0:T(8,128)(2,1)S(1)} %convolution_convert_fusion.2, ...), kind=kOutput, calls=%fused_computation.26 | convolution fusion | flops 1061371904 | bytes 11933825 | tf_op jit(solution)/shard_map/dot_general | solution.py:90
  56.4 1.2 collective-permute-start.2
  57.7 1.6 fusion.21
  59.2 1.0 collective-permute-start.4
  60.2 1.2 collective-permute-start.3
  61.4 98.5 %collective-permute-done.2 = s32[1024]{0:T(1024)S(1)} collective-permute-done((s32[1024]{0:T(1024)S(1)}, s32[1024]{0:T(1024)S(1)}, u32[]{:S(2)}, u32[]{:S(2)}) %collective-permute-start.2) | collective-permute-done | bytes 4128 | tf_op jit(solution)/shard_map/ppermute | solution.py:11
  160.1 3.9 %fusion.61 = f32[128,3584]{1,0:T(8,128)S(1)} fusion(bf16[832,3584]{1,0:T(8,128)(2,1)} %collective-permute-done.5, pred[128,896]{1,0:T(32,128)(4,1)S(1)} %broadcast_compare_fusion), kind=kOutput, calls=%fused_computation.67 | convolution fusion | flops 763363328 | bytes 7913472 | tf_op jit(solution)/shard_map/dot_general | solution.py:103
  164.0 5.6 %collective-permute-done.4 = bf16[64,3584]{1,0:T(8,128)(2,1)S(1)} collective-permute-done((bf16[64,3584]{1,0:T(8,128)(2,1)S(1)}, bf16[64,3584]{1,0:T(8,128)(2,1)S(1)}, u32[]{:S(2)}, u32[]{:S(2)}) %collective-permute-start.4) | collective-permute-done | bytes 458784 | tf_op jit(solution)/shard_map/ppermute | solution.py:11
  169.6 19.7 %collective-permute-done.3 = bf16[128,3584]{1,0:T(8,128)(2,1)S(1)} collective-permute-done((bf16[128,3584]{1,0:T(8,128)(2,1)}, bf16[128,3584]{1,0:T(8,128)(2,1)S(1)}, u32[]{:S(2)}, u32[]{:S(2)}) %collective-permute-start.3) | collective-permute-done | bytes 917536 | tf_op jit(solution)/shard_map/ppermute | solution.py:11
  189.3 8.7 %fusion.8 = bf16[1,1024,3584]{2,1,0:T(8,128)(2,1)} fusion(bf16[128,3584]{1,0:T(8,128)(2,1)S(1)} %collective-permute-done.3, bf16[832,3584]{1,0:T(8,128)(2,1)} %collective-permute-done.5, bf16[64,3584]{1,0:T(8,128)(2,1)S(1)} %collective-permute-done.4, pred[1024]{0:T(1024)(128)(4,1)S(1)} %broadcast_compare_fusion.1, s32[1024]{0:T(1024)S(1)} %fusion.86), kind=kOutput, calls=%fused_computation.11 | convolution fusion | flops 969015296 | bytes 14685184 | tf_op jit(solution)/shard_map/dot_general | solution.py:99
  198.0 1.3 bitcast_dynamic-update-slice_fusion
  (46 shorter events, 4.6 us)
Async XLA Ops:
  0.0 29.6 %copy-start = (bf16[1,3584,128]{2,1,0:T(8,128)(2,1)S(1)}, bf16[1,3584,128]{2,1,0:T(8,128)(2,1)}, u32[]{:S(2)}) copy-start(bf16[1,3584,128]{2,1,0:T(8,128)(2,1)} %param.9) | copy-start | bytes 2752516
  0.9 5.7 %copy-start.2 = (f32[1,3584]{1,0:T(1,128)S(1)}, f32[1,3584]{1,0:T(1,128)}, u32[]{:S(2)}) copy-start(f32[1,3584]{1,0:T(1,128)} %param.8) | copy-start | bytes 43012
  13.1 23.1 %collective-permute-start = (bf16[128,3584]{1,0:T(8,128)(2,1)}, bf16[128,3584]{1,0:T(8,128)(2,1)}, u32[]{:S(2)}, u32[]{:S(2)}) collective-permute-start(bf16[128,3584]{1,0:T(8,128)(2,1)} %fusion.17), channel_id=1, source_target_pairs={{0,1},{1,0},{2,3},{3,2},{4,5},{5,4},{6,7},{7,6},{8,9},{9,8},{10,11... | collective-permute-start | bytes 2752520 | tf_op jit(solution)/shard_map/ppermute | solution.py:15
  16.5 7.0 %copy-start.1 = (s32[1,1,1024,8]{2,3,1,0:T(8,128)S(1)}, s32[1,1,1024,8]{2,3,1,0:T(8,128)}, u32[]{:S(2)}) copy-start(s32[1,1,1024,8]{2,3,1,0:T(8,128)} %param.13) | copy-start | bytes 98308
  22.1 138.0 %collective-permute-start.5 = (bf16[832,3584]{1,0:T(8,128)(2,1)}, bf16[832,3584]{1,0:T(8,128)(2,1)}, u32[]{:S(2)}, u32[]{:S(2)}) collective-permute-start(bf16[832,3584]{1,0:T(8,128)(2,1)} %bitcast_select_fusion), channel_id=1, source_target_pairs={{0,2},{2,4},{4,6},{6,8},{8,10},{10,12},{12,14},{14,16},{16,18},{18... | collective-permute-start | bytes 17891336 | tf_op jit(solution)/shard_map/ppermute | solution.py:11
  29.6 6.6 %copy-start.3 = (bf16[1,3584,512]{2,1,0:T(8,128)(2,1)S(1)}, bf16[1,3584,512]{2,1,0:T(8,128)(2,1)}, u32[]{:S(2)}) copy-start(bf16[1,3584,512]{2,1,0:T(8,128)(2,1)} %param.10) | copy-start | bytes 11010052
  46.8 2.6 %collective-permute-start.1 = (bf16[128,3584]{1,0:T(8,128)(2,1)S(1)}, bf16[128,3584]{1,0:T(8,128)(2,1)S(1)}, u32[]{:S(2)}, u32[]{:S(2)}) collective-permute-start(bf16[128,3584]{1,0:T(8,128)(2,1)S(1)} %broadcast_select_fusion), channel_id=1, source_target_pairs={{0,1},{1,0},{2,3},{3,2},{4,5},{5,4},{6,7},{7,6},{8,9},{9,8},{10,11... | collective-permute-start | bytes 2752520 | tf_op jit(solution)/shard_map/ppermute | solution.py:15
  49.4 0.9 copy-start.4
  56.4 103.5 %collective-permute-start.2 = (s32[1024]{0:T(1024)S(1)}, s32[1024]{0:T(1024)S(1)}, u32[]{:S(2)}, u32[]{:S(2)}) collective-permute-start(s32[1024]{0:T(1024)S(1)} %pad_add_fusion), channel_id=1, source_target_pairs={{0,2},{2,4},{4,6},{6,8},{8,10},{10,12},{12,14},{14,16},{16,18},{18... | collective-permute-start | bytes 12296 | tf_op jit(solution)/shard_map/ppermute | solution.py:11
  59.2 110.4 %collective-permute-start.4 = (bf16[64,3584]{1,0:T(8,128)(2,1)S(1)}, bf16[64,3584]{1,0:T(8,128)(2,1)S(1)}, u32[]{:S(2)}, u32[]{:S(2)}) collective-permute-start(bf16[64,3584]{1,0:T(8,128)(2,1)S(1)} %fusion.21), channel_id=1, source_target_pairs={{0,2},{2,4},{4,6},{6,8},{8,10},{10,12},{12,14},{14,16},{16,18},{18... | collective-permute-start | bytes 1376264 | tf_op jit(solution)/shard_map/ppermute | solution.py:11
  60.2 129.1 %collective-permute-start.3 = (bf16[128,3584]{1,0:T(8,128)(2,1)}, bf16[128,3584]{1,0:T(8,128)(2,1)S(1)}, u32[]{:S(2)}, u32[]{:S(2)}) collective-permute-start(bf16[128,3584]{1,0:T(8,128)(2,1)} %fusion.20), channel_id=1, source_target_pairs={{0,2},{2,4},{4,6},{6,8},{8,10},{10,12},{12,14},{14,16},{16,18},{18... | collective-permute-start | bytes 2752520 | tf_op jit(solution)/shard_map/ppermute | solution.py:11

commit v3 on v2

--- a/solution.py
+++ b/solution.py
@@ -99,10 +99,10 @@
                     jnp.dot(back_top, second, preferred_element_type=jnp.float32).astype(jnp.bfloat16),
                     jnp.concatenate(moved_first + [second], axis=0))
     back_tail = (tail_mate[:, None] == row_iota[None, :bulk]).astype(jnp.bfloat16)
-    low = jnp.where((tail_mate >= 0)[:, None],
-                    sum(jnp.dot(back_tail[:, a:b], part, preferred_element_type=jnp.float32)
-                        for (a, b), part in zip(cuts, moved_first)).astype(jnp.bfloat16),
-                    second)
+    raw_low = sum(jnp.dot(back_tail[:, a:b], part, preferred_element_type=jnp.float32)
+                  for (a, b), part in zip(cuts, moved_first)).astype(jnp.bfloat16)
+    raw_low = lax.optimization_barrier(raw_low)
+    low = jnp.where((tail_mate >= 0)[:, None], raw_low, second)
     out = lax.dynamic_update_slice(out, low, (bulk, 0))
     return out[None]
 

time: 200 us -> 199 us (level)
  no operation moved by 1% of the time
where the time goes in v3:
time: 199 us
  waiting for transfers between devices  124 us (62%)
  matrix products  51 us (26%)
  other arithmetic  15.6 us (8%)
  starting transfers between devices  6.48 us (3%)
    ppermute x4, waiting for transfers between devices, passed_along(): lax.ppermute(x, axis, [(i, (i + by) % devices) for i in range(devices)])  123 us
    dot_general x1, matrix products, local(): jnp.dot(back_top, second, preferred_element_type=jnp.float32)  8.56 us
    dot_general x2, matrix products, local(): jnp.dot(pairs[a:b].astype(jnp.bfloat16), current[bulk:], preferred_elemen...  7.18 us
    dot_general x1, matrix products, local(): jnp.dot(normed, table, preferred_element_type=jnp.float32)  6.54 us
    dot_general x1, matrix products, expert_part(): partial_out = jnp.dot(active, down_dev, preferred_element_type=jnp.float32)  6.51 us
    dot_general x1, matrix products, local(): jnp.dot(onehot, normed, preferred_element_type=jnp.float32)  6.46 us
    dot_general x1, matrix products, local(): jnp.dot(carry, new_rows, preferred_element_type=jnp.float32)  6.14 us
    reduce_sum x1, other arithmetic, local(): jnp.sum((ids[:, :, None] == expert_iota[None, None, :]).astype(jnp.float3...  5.75 us
  transfers between devices with their start and end apart: 6, of which 4 were waited for; matrix products, arithmetic and copies ran while one was open for 22% of the time, Pallas kernels for 0%

profile of v3, /device:TPU:1, one launch (start us, length us, event | category | flops | bytes accessed | tf_op | source)
XLA Modules:
  0.0 199.1 jit_solution(9837698721688184087)
XLA Ops:
  0.0 0.9 convert_reduce_fusion.1
  2.0 4.6 %fusion = f32[1024]{0:T(1024)S(1)} fusion(bf16[1,1024,3584]{2,1,0:T(8,128)(2,1)} %param.7), kind=kLoop, calls=%fused_computation.2 | loop fusion | flops 11009024 | bytes 7344128 | tf_op jit(solution)/shard_map/reduce_sum | solution.py:67
  6.7 6.5 %fusion.17 = bf16[128,3584]{1,0:T(8,128)(2,1)} fusion(bf16[1,1024,3584]{2,1,0:T(8,128)(2,1)} %param.7, f32[3584]{0:T(1024)S(1)} %reduce.2, f32[1024]{0:T(1024)S(1)} %add_rsqrt_fusion, s32[1024]{0:T(1024)S(1)} %convert_element_type.80, pred[1024]{0:T(1024)(128)(4,1)S(1)} %get-tuple-element.16), kind=kOutput, calls=%fused_computation.25 | convolution fusion | flops 954925056 | bytes 8281088 | tf_op jit(solution)/shard_map/dot_general | solution.py:75
  13.1 1.4 collective-permute-start
  16.5 5.6 %bitcast_select_fusion = bf16[832,3584]{1,0:T(8,128)(2,1)} fusion(bf16[1,1024,3584]{2,1,0:T(8,128)(2,1)} %param.7, pred[832]{0:T(1024)(128)(4,1)S(1)} %slice.115, pred[896,128]{1,0:T(32,128)(4,1)S(1)} %get-tuple-element.14), kind=kOutput, calls=%fused_computation.20 | convolution fusion | flops 769327104 | bytes 12952576 | tf_op jit(solution)/shard_map/dot_general | solution.py:60
  22.1 1.3 collective-permute-start.5
  23.6 5.7 %convert_reduce_fusion = f32[1024,128]{1,0:T(8,128)S(1)} fusion(s32[1024,8]{1,0:T(8,128)S(1)} %copy.10), kind=kLoop, calls=%fused_computation.29 | loop fusion | flops 3014656 | bytes 557056 | tf_op jit(solution)/shard_map/reduce_sum | solution.py:71
  29.6 6.5 %multiply_reduce_fusion = (f32[1024]{0:T(1024)S(1)}, f32[1024,128]{0,1:T(8,128)}) fusion(f32[1024,128]{0,1:T(8,128)S(1)} %copy.11, bf16[1,3584,128]{2,1,0:T(8,128)(2,1)S(1)} %copy-done, bf16[1,1024,3584]{2,1,0:T(8,128)(2,1)} %param.7, f32[3584]{0:T(1024)S(1)} %reduce.2, f32[1024]{0:T(1024)S(1)} %add_rsqrt_fusion), kind=kOutput, calls=%fused_computation.60 | convolution fusion | flops 954858496 | bytes 9328640 | tf_op jit(solution)/shard_map/dot_general | solution.py:69
  36.2 4.1 %fusion.27 = f32[256,512]{1,0:T(8,128)} fusion(bf16[1,3584,512]{2,1,0:T(8,128)(2,1)S(1)} %copy-done.3, bf16[128,3584]{1,0:T(8,128)(2,1)} %collective-permute-done, bf16[128,3584]{1,0:T(8,128)(2,1)} %fusion.17, pred[]{:T(512)S(6)} %eq.106), kind=kOutput, calls=%fused_computation.37 | convolution fusion | flops 947781632 | bytes 6029313 | tf_op jit(solution)/shard_map/dot_general | solution.py:19
  40.2 6.5 %convolution_convert_fusion.2 = bf16[256,3584]{1,0:T(8,128)(2,1)S(1)} fusion(bf16[1,512,3584]{2,1,0:T(8,128)(2,1)} %param.12, f32[256,512]{1,0:T(8,128)} %fusion.27, bf16[1,3584,512]{2,1,0:T(8,128)(2,1)} %param.11, bf16[128,3584]{1,0:T(8,128)(2,1)} %collective-permute-done, bf16[128,3584]{1,0:T(8,128)(2,1)} %fusion.17, pred[]{:T(512)S(6)} %eq.106), kind=kOutput, calls=%fused_computation.21 | convolution fusion | flops 1889009664 | bytes 11534337 | tf_op jit(solution)/shard_map/dot_general | solution.py:22
  47.2 0.8 slice_multiply_fusion
  48.4 1.0 collective-permute-done.1
  49.4 0.9 copy-done.4
  50.4 6.1 %fusion.20 = bf16[128,3584]{1,0:T(8,128)(2,1)} fusion(bf16[128,3584]{1,0:T(8,128)(2,1)} %copy-done.4, f32[128]{0:T(128)S(1)} %convolution_bitcast_fusion, pred[128]{0:T(512)(128)(4,1)S(1)} %get-tuple-element.12, pred[]{:T(512)S(6)} %eq.106, bf16[1,1024,3584]{2,1,0:T(8,128)(2,1)} %param.7, bf16[256,3584]{1,0:T(8,128)(2,1)S(1)} %convolution_convert_fusion.2, ...), kind=kOutput, calls=%fused_computation.26 | convolution fusion | flops 1061371904 | bytes 11933825 | tf_op jit(solution)/shard_map/dot_general | solution.py:90
  56.5 1.2 collective-permute-start.2
  57.7 1.6 fusion.21
  59.3 1.0 collective-permute-start.4
  60.3 1.2 collective-permute-start.3
  61.5 98.4 %collective-permute-done.2 = s32[1024]{0:T(1024)S(1)} collective-permute-done((s32[1024]{0:T(1024)S(1)}, s32[1024]{0:T(1024)S(1)}, u32[]{:S(2)}, u32[]{:S(2)}) %collective-permute-start.2) | collective-permute-done | bytes 4128 | tf_op jit(solution)/shard_map/ppermute | solution.py:11
  160.1 3.9 %fusion.61 = f32[128,3584]{1,0:T(8,128)S(1)} fusion(bf16[832,3584]{1,0:T(8,128)(2,1)} %collective-permute-done.5, pred[128,896]{1,0:T(32,128)(4,1)S(1)} %broadcast_compare_fusion), kind=kOutput, calls=%fused_computation.67 | convolution fusion | flops 763363328 | bytes 7913472 | tf_op jit(solution)/shard_map/dot_general | solution.py:102
  164.0 5.6 %collective-permute-done.4 = bf16[64,3584]{1,0:T(8,128)(2,1)S(1)} collective-permute-done((bf16[64,3584]{1,0:T(8,128)(2,1)S(1)}, bf16[64,3584]{1,0:T(8,128)(2,1)S(1)}, u32[]{:S(2)}, u32[]{:S(2)}) %collective-permute-start.4) | collective-permute-done | bytes 458784 | tf_op jit(solution)/shard_map/ppermute | solution.py:11
  170.0 19.3 %collective-permute-done.3 = bf16[128,3584]{1,0:T(8,128)(2,1)S(1)} collective-permute-done((bf16[128,3584]{1,0:T(8,128)(2,1)}, bf16[128,3584]{1,0:T(8,128)(2,1)S(1)}, u32[]{:S(2)}, u32[]{:S(2)}) %collective-permute-start.3) | collective-permute-done | bytes 917536 | tf_op jit(solution)/shard_map/ppermute | solution.py:11
  189.3 8.6 %fusion.8 = bf16[1,1024,3584]{2,1,0:T(8,128)(2,1)} fusion(bf16[128,3584]{1,0:T(8,128)(2,1)S(1)} %collective-permute-done.3, bf16[832,3584]{1,0:T(8,128)(2,1)} %collective-permute-done.5, bf16[64,3584]{1,0:T(8,128)(2,1)S(1)} %collective-permute-done.4, pred[1024]{0:T(1024)(128)(4,1)S(1)} %broadcast_compare_fusion.1, s32[1024]{0:T(1024)S(1)} %fusion.84), kind=kOutput, calls=%fused_computation.11 | convolution fusion | flops 969015296 | bytes 14685184 | tf_op jit(solution)/shard_map/dot_general | solution.py:99
  197.9 1.2 bitcast_dynamic-update-slice_fusion
  (47 shorter events, 5.0 us)
Async XLA Ops:
  0.0 29.6 %copy-start = (bf16[1,3584,128]{2,1,0:T(8,128)(2,1)S(1)}, bf16[1,3584,128]{2,1,0:T(8,128)(2,1)}, u32[]{:S(2)}) copy-start(bf16[1,3584,128]{2,1,0:T(8,128)(2,1)} %param.9) | copy-start | bytes 2752516
  0.9 5.7 %copy-start.2 = (f32[1,3584]{1,0:T(1,128)S(1)}, f32[1,3584]{1,0:T(1,128)}, u32[]{:S(2)}) copy-start(f32[1,3584]{1,0:T(1,128)} %param.8) | copy-start | bytes 43012
  13.1 23.1 %collective-permute-start = (bf16[128,3584]{1,0:T(8,128)(2,1)}, bf16[128,3584]{1,0:T(8,128)(2,1)}, u32[]{:S(2)}, u32[]{:S(2)}) collective-permute-start(bf16[128,3584]{1,0:T(8,128)(2,1)} %fusion.17), channel_id=1, source_target_pairs={{0,1},{1,0},{2,3},{3,2},{4,5},{5,4},{6,7},{7,6},{8,9},{9,8},{10,11... | collective-permute-start | bytes 2752520 | tf_op jit(solution)/shard_map/ppermute | solution.py:15
  16.5 6.9 %copy-start.1 = (s32[1,1,1024,8]{2,3,1,0:T(8,128)S(1)}, s32[1,1,1024,8]{2,3,1,0:T(8,128)}, u32[]{:S(2)}) copy-start(s32[1,1,1024,8]{2,3,1,0:T(8,128)} %param.13) | copy-start | bytes 98308
  22.1 138.0 %collective-permute-start.5 = (bf16[832,3584]{1,0:T(8,128)(2,1)}, bf16[832,3584]{1,0:T(8,128)(2,1)}, u32[]{:S(2)}, u32[]{:S(2)}) collective-permute-start(bf16[832,3584]{1,0:T(8,128)(2,1)} %bitcast_select_fusion), channel_id=1, source_target_pairs={{0,2},{2,4},{4,6},{6,8},{8,10},{10,12},{12,14},{14,16},{16,18},{18... | collective-permute-start | bytes 17891336 | tf_op jit(solution)/shard_map/ppermute | solution.py:11
  29.6 6.6 %copy-start.3 = (bf16[1,3584,512]{2,1,0:T(8,128)(2,1)S(1)}, bf16[1,3584,512]{2,1,0:T(8,128)(2,1)}, u32[]{:S(2)}) copy-start(bf16[1,3584,512]{2,1,0:T(8,128)(2,1)} %param.10) | copy-start | bytes 11010052
  46.9 2.6 %collective-permute-start.1 = (bf16[128,3584]{1,0:T(8,128)(2,1)S(1)}, bf16[128,3584]{1,0:T(8,128)(2,1)S(1)}, u32[]{:S(2)}, u32[]{:S(2)}) collective-permute-start(bf16[128,3584]{1,0:T(8,128)(2,1)S(1)} %broadcast_select_fusion), channel_id=1, source_target_pairs={{0,1},{1,0},{2,3},{3,2},{4,5},{5,4},{6,7},{7,6},{8,9},{9,8},{10,11... | collective-permute-start | bytes 2752520 | tf_op jit(solution)/shard_map/ppermute | solution.py:15
  49.4 0.9 copy-start.4
  56.5 103.4 %collective-permute-start.2 = (s32[1024]{0:T(1024)S(1)}, s32[1024]{0:T(1024)S(1)}, u32[]{:S(2)}, u32[]{:S(2)}) collective-permute-start(s32[1024]{0:T(1024)S(1)} %pad_add_fusion), channel_id=1, source_target_pairs={{0,2},{2,4},{4,6},{6,8},{8,10},{10,12},{12,14},{14,16},{16,18},{18... | collective-permute-start | bytes 12296 | tf_op jit(solution)/shard_map/ppermute | solution.py:11
  59.3 110.3 %collective-permute-start.4 = (bf16[64,3584]{1,0:T(8,128)(2,1)S(1)}, bf16[64,3584]{1,0:T(8,128)(2,1)S(1)}, u32[]{:S(2)}, u32[]{:S(2)}) collective-permute-start(bf16[64,3584]{1,0:T(8,128)(2,1)S(1)} %fusion.21), channel_id=1, source_target_pairs={{0,2},{2,4},{4,6},{6,8},{8,10},{10,12},{12,14},{14,16},{16,18},{18... | collective-permute-start | bytes 1376264 | tf_op jit(solution)/shard_map/ppermute | solution.py:11
  60.3 129.0 %collective-permute-start.3 = (bf16[128,3584]{1,0:T(8,128)(2,1)}, bf16[128,3584]{1,0:T(8,128)(2,1)S(1)}, u32[]{:S(2)}, u32[]{:S(2)}) collective-permute-start(bf16[128,3584]{1,0:T(8,128)(2,1)} %fusion.20), channel_id=1, source_target_pairs={{0,2},{2,4},{4,6},{6,8},{8,10},{10,12},{12,14},{14,16},{16,18},{18... | collective-permute-start | bytes 2752520 | tf_op jit(solution)/shard_map/ppermute | solution.py:11

commit v4 on v3

--- a/solution.py
+++ b/solution.py
@@ -93,11 +93,15 @@
     second = passed_along(second, "section", 1)
     mate = passed_along(mate, "section", 1)
     tail_mate = mate[bulk:]
-    top_mate = jnp.where(row_iota < bulk, mate, -1)
-    back_top = (top_mate[:, None] == tail_iota[None, :]).astype(jnp.bfloat16)
-    out = jnp.where((top_mate >= 0)[:, None],
-                    jnp.dot(back_top, second, preferred_element_type=jnp.float32).astype(jnp.bfloat16),
-                    jnp.concatenate(moved_first + [second], axis=0))
+
+    def with_holes(a, b, part):
+        ties = (mate[a:b, None] == tail_iota[None, :]).astype(jnp.bfloat16)
+        filled = jnp.dot(ties, second, preferred_element_type=jnp.float32).astype(jnp.bfloat16)
+        return jnp.where((mate[a:b] >= 0)[:, None], filled, part)
+
+    (a0, b0), (a1, b1) = cuts
+    out = jnp.pad(with_holes(a1, b1, moved_first[1]), ((a1, rows - b1), (0, 0)))
+    out = lax.dynamic_update_slice(out, with_holes(a0, b0, moved_first[0]), (a0, 0))
     back_tail = (tail_mate[:, None] == row_iota[None, :bulk]).astype(jnp.bfloat16)
     raw_low = sum(jnp.dot(back_tail[:, a:b], part, preferred_element_type=jnp.float32)
                   for (a, b), part in zip(cuts, moved_first)).astype(jnp.bfloat16)

time: 199 us -> 200 us (level)
  local copies, waits for them, and re-layouts: 1.5 us -> 5.08 us
  matrix products: 51 us -> 47.6 us
    broadcast_in_dim x0 -> x1, local copies, waits for them, and re-layouts: none -> 3.52 us  [local(): return out[None]]
    dot_general x1 -> x2, matrix products: 8.56 us -> 5.21 us  [with_holes(): jnp.dot(ties, second, preferred_element_type=jnp.float32)]
where the time goes in v4:
time: 200 us; the launch traced here: 199 us
  waiting for transfers between devices  124 us (62%)
  matrix products  47.6 us (24%)
  other arithmetic  15.6 us (8%)
  starting transfers between devices  6.46 us (3%)
  local copies, waits for them, and re-layouts  5.08 us (3%)
    ppermute x4, waiting for transfers between devices, passed_along(): lax.ppermute(x, axis, [(i, (i + by) % devices) for i in range(devices)])  123 us
    dot_general x2, matrix products, local(): jnp.dot(pairs[a:b].astype(jnp.bfloat16), current[bulk:], preferred_elemen...  7.18 us
    dot_general x1, matrix products, local(): jnp.dot(normed, table, preferred_element_type=jnp.float32)  6.54 us
    dot_general x1, matrix products, expert_part(): partial_out = jnp.dot(active, down_dev, preferred_element_type=jnp.float32)  6.53 us
    dot_general x1, matrix products, local(): jnp.dot(onehot, normed, preferred_element_type=jnp.float32)  6.44 us
    dot_general x1, matrix products, local(): jnp.dot(carry, new_rows, preferred_element_type=jnp.float32)  6.15 us
    reduce_sum x1, other arithmetic, local(): jnp.sum((ids[:, :, None] == expert_iota[None, None, :]).astype(jnp.float3...  5.75 us
    dot_general x2, matrix products, with_holes(): jnp.dot(ties, second, preferred_element_type=jnp.float32)  5.21 us
  transfers between devices with their start and end apart: 6, of which 4 were waited for; matrix products, arithmetic and copies ran while one was open for 22% of the time, Pallas kernels for 0%

profile of v4, /device:TPU:1, one launch (start us, length us, event | category | flops | bytes accessed | tf_op | source)
XLA Modules:
  0.0 199.3 jit_solution(17699177427467497820)
XLA Ops:
  2.0 4.6 %fusion = f32[1024]{0:T(1024)S(1)} fusion(bf16[1,1024,3584]{2,1,0:T(8,128)(2,1)} %param.7), kind=kLoop, calls=%fused_computation.2 | loop fusion | flops 11009024 | bytes 7344128 | tf_op jit(solution)/shard_map/reduce_sum | solution.py:67
  6.7 6.4 %fusion.16 = bf16[128,3584]{1,0:T(8,128)(2,1)} fusion(bf16[1,1024,3584]{2,1,0:T(8,128)(2,1)} %param.7, f32[3584]{0:T(1024)S(1)} %reduce.2, f32[1024]{0:T(1024)S(1)} %add_rsqrt_fusion, s32[1024]{0:T(1024)S(1)} %convert_element_type.86, pred[1024]{0:T(1024)(128)(4,1)S(1)} %get-tuple-element.16), kind=kOutput, calls=%fused_computation.25 | convolution fusion | flops 954925056 | bytes 8281088 | tf_op jit(solution)/shard_map/dot_general | solution.py:75
  13.1 1.4 collective-permute-start
  16.5 5.6 %bitcast_select_fusion = bf16[832,3584]{1,0:T(8,128)(2,1)} fusion(bf16[1,1024,3584]{2,1,0:T(8,128)(2,1)} %param.7, pred[832]{0:T(1024)(128)(4,1)S(1)} %slice.120, pred[896,128]{1,0:T(32,128)(4,1)S(1)} %get-tuple-element.14), kind=kOutput, calls=%fused_computation.19 | convolution fusion | flops 769327104 | bytes 12952576 | tf_op jit(solution)/shard_map/dot_general | solution.py:60
  22.1 1.3 collective-permute-start.4
  23.6 5.7 %convert_reduce_fusion = f32[1024,128]{1,0:T(8,128)S(1)} fusion(s32[1024,8]{1,0:T(8,128)S(1)} %copy.10), kind=kLoop, calls=%fused_computation.30 | loop fusion | flops 3014656 | bytes 557056 | tf_op jit(solution)/shard_map/reduce_sum | solution.py:71
  29.6 6.5 %multiply_reduce_fusion = (f32[1024]{0:T(1024)S(1)}, f32[1024,128]{0,1:T(8,128)}) fusion(f32[1024,128]{0,1:T(8,128)S(1)} %copy.11, bf16[1,3584,128]{2,1,0:T(8,128)(2,1)S(1)} %copy-done, bf16[1,1024,3584]{2,1,0:T(8,128)(2,1)} %param.7, f32[3584]{0:T(1024)S(1)} %reduce.2, f32[1024]{0:T(1024)S(1)} %add_rsqrt_fusion), kind=kOutput, calls=%fused_computation.60 | convolution fusion | flops 954858496 | bytes 9328640 | tf_op jit(solution)/shard_map/dot_general | solution.py:69
  36.2 4.1 %fusion.26 = f32[256,512]{1,0:T(8,128)} fusion(bf16[1,3584,512]{2,1,0:T(8,128)(2,1)S(1)} %copy-done.4, bf16[128,3584]{1,0:T(8,128)(2,1)} %collective-permute-done, bf16[128,3584]{1,0:T(8,128)(2,1)} %fusion.16, pred[]{:T(512)S(6)} %eq.119), kind=kOutput, calls=%fused_computation.38 | convolution fusion | flops 947781632 | bytes 6029313 | tf_op jit(solution)/shard_map/dot_general | solution.py:19
  40.2 6.5 %convolution_convert_fusion.2 = bf16[256,3584]{1,0:T(8,128)(2,1)S(1)} fusion(bf16[1,512,3584]{2,1,0:T(8,128)(2,1)} %param.12, f32[256,512]{1,0:T(8,128)} %fusion.26, bf16[1,3584,512]{2,1,0:T(8,128)(2,1)} %param.11, bf16[128,3584]{1,0:T(8,128)(2,1)} %collective-permute-done, bf16[128,3584]{1,0:T(8,128)(2,1)} %fusion.16, pred[]{:T(512)S(6)} %eq.119), kind=kOutput, calls=%fused_computation.21 | convolution fusion | flops 1889009664 | bytes 11534337 | tf_op jit(solution)/shard_map/dot_general | solution.py:22
  48.4 1.0 collective-permute-done.1
  49.4 0.9 copy-done.5
  50.4 6.2 %fusion.19 = bf16[128,3584]{1,0:T(8,128)(2,1)} fusion(bf16[128,3584]{1,0:T(8,128)(2,1)} %copy-done.5, f32[128]{0:T(128)S(1)} %convolution_bitcast_fusion, pred[128]{0:T(512)(128)(4,1)S(1)} %get-tuple-element.12, pred[]{:T(512)S(6)} %eq.119, bf16[1,1024,3584]{2,1,0:T(8,128)(2,1)} %param.7, bf16[256,3584]{1,0:T(8,128)(2,1)S(1)} %convolution_convert_fusion.2, ...), kind=kOutput, calls=%fused_computation.26 | convolution fusion | flops 1061371904 | bytes 11933825 | tf_op jit(solution)/shard_map/dot_general | solution.py:90
  56.5 1.2 collective-permute-start.2
  57.7 1.6 fusion.20
  59.3 1.0 collective-permute-start.5
  60.3 1.2 collective-permute-start.3
  61.5 98.4 %collective-permute-done.2 = s32[1024]{0:T(1024)S(1)} collective-permute-done((s32[1024]{0:T(1024)S(1)}, s32[1024]{0:T(1024)S(1)}, u32[]{:S(2)}, u32[]{:S(2)}) %collective-permute-start.2) | collective-permute-done | bytes 4128 | tf_op jit(solution)/shard_map/ppermute | solution.py:11
  160.2 3.9 %fusion.60 = f32[128,3584]{1,0:T(8,128)S(1)} fusion(bf16[832,3584]{1,0:T(8,128)(2,1)} %collective-permute-done.4, pred[128,896]{1,0:T(32,128)(4,1)S(1)} %broadcast_compare_fusion), kind=kOutput, calls=%fused_computation.68 | convolution fusion | flops 763363328 | bytes 7913472 | tf_op jit(solution)/shard_map/dot_general | solution.py:106
  164.1 5.5 %collective-permute-done.5 = bf16[64,3584]{1,0:T(8,128)(2,1)S(1)} collective-permute-done((bf16[64,3584]{1,0:T(8,128)(2,1)S(1)}, bf16[64,3584]{1,0:T(8,128)(2,1)S(1)}, u32[]{:S(2)}, u32[]{:S(2)}) %collective-permute-start.5) | collective-permute-done | bytes 458784 | tf_op jit(solution)/shard_map/ppermute | solution.py:11
  170.0 19.3 %collective-permute-done.3 = bf16[128,3584]{1,0:T(8,128)(2,1)S(1)} collective-permute-done((bf16[128,3584]{1,0:T(8,128)(2,1)}, bf16[128,3584]{1,0:T(8,128)(2,1)S(1)}, u32[]{:S(2)}, u32[]{:S(2)}) %collective-permute-start.3) | collective-permute-done | bytes 917536 | tf_op jit(solution)/shard_map/ppermute | solution.py:11
  189.3 4.1 %broadcast_select_fusion = bf16[832,3584]{1,0:T(8,128)(2,1)S(1)} fusion(bf16[832,3584]{1,0:T(8,128)(2,1)} %collective-permute-done.4, pred[832]{0:T(1024)(128)(4,1)S(1)} %broadcast_compare_fusion.1, bf16[128,3584]{1,0:T(8,128)(2,1)S(1)} %collective-permute-done.3, s32[832]{0:T(1024)S(1)} %slice.119), kind=kOutput, calls=%fused_computation.20 | convolution fusion | flops 769433600 | bytes 12849216 | tf_op jit(solution)/shard_map/dot_general | solution.py:99
  193.4 3.5 %pad_bitcast_fusion = bf16[1,1024,3584]{2,1,0:T(8,128)(2,1)} fusion(bf16[832,3584]{1,0:T(8,128)(2,1)S(1)} %broadcast_select_fusion), kind=kLoop, calls=%fused_computation.12 | loop fusion | bytes 13303808 | tf_op jit(solution)/shard_map/broadcast_in_dim | solution.py:111
  196.9 1.1 bitcast_dynamic-update-slice_fusion.1
  198.0 1.2 bitcast_dynamic-update-slice_fusion
  (54 shorter events, 6.7 us)
Async XLA Ops:
  0.0 29.6 %copy-start = (bf16[1,3584,128]{2,1,0:T(8,128)(2,1)S(1)}, bf16[1,3584,128]{2,1,0:T(8,128)(2,1)}, u32[]{:S(2)}) copy-start(bf16[1,3584,128]{2,1,0:T(8,128)(2,1)} %param.9) | copy-start | bytes 2752516
  2.0 4.6 %copy-start.3 = (f32[1,3584]{1,0:T(1,128)S(1)}, f32[1,3584]{1,0:T(1,128)}, u32[]{:S(2)}) copy-start(f32[1,3584]{1,0:T(1,128)} %param.8) | copy-start | bytes 43012
  13.1 23.1 %collective-permute-start = (bf16[128,3584]{1,0:T(8,128)(2,1)}, bf16[128,3584]{1,0:T(8,128)(2,1)}, u32[]{:S(2)}, u32[]{:S(2)}) collective-permute-start(bf16[128,3584]{1,0:T(8,128)(2,1)} %fusion.16), channel_id=1, source_target_pairs={{0,1},{1,0},{2,3},{3,2},{4,5},{5,4},{6,7},{7,6},{8,9},{9,8},{10,11... | collective-permute-start | bytes 2752520 | tf_op jit(solution)/shard_map/ppermute | solution.py:15
  16.5 7.0 %copy-start.1 = (s32[1,1,1024,8]{2,3,1,0:T(8,128)S(1)}, s32[1,1,1024,8]{2,3,1,0:T(8,128)}, u32[]{:S(2)}) copy-start(s32[1,1,1024,8]{2,3,1,0:T(8,128)} %param.13) | copy-start | bytes 98308
  22.1 138.1 %collective-permute-start.4 = (bf16[832,3584]{1,0:T(8,128)(2,1)}, bf16[832,3584]{1,0:T(8,128)(2,1)}, u32[]{:S(2)}, u32[]{:S(2)}) collective-permute-start(bf16[832,3584]{1,0:T(8,128)(2,1)} %bitcast_select_fusion), channel_id=1, source_target_pairs={{0,2},{2,4},{4,6},{6,8},{8,10},{10,12},{12,14},{14,16},{16,18},{18... | collective-permute-start | bytes 17891336 | tf_op jit(solution)/shard_map/ppermute | solution.py:11
  29.6 6.6 %copy-start.4 = (bf16[1,3584,512]{2,1,0:T(8,128)(2,1)S(1)}, bf16[1,3584,512]{2,1,0:T(8,128)(2,1)}, u32[]{:S(2)}) copy-start(bf16[1,3584,512]{2,1,0:T(8,128)(2,1)} %param.10) | copy-start | bytes 11010052
  46.9 2.6 %collective-permute-start.1 = (bf16[128,3584]{1,0:T(8,128)(2,1)S(1)}, bf16[128,3584]{1,0:T(8,128)(2,1)S(1)}, u32[]{:S(2)}, u32[]{:S(2)}) collective-permute-start(bf16[128,3584]{1,0:T(8,128)(2,1)S(1)} %broadcast_select_fusion.1), channel_id=1, source_target_pairs={{0,1},{1,0},{2,3},{3,2},{4,5},{5,4},{6,7},{7,6},{8,9},{9,8},{10,11... | collective-permute-start | bytes 2752520 | tf_op jit(solution)/shard_map/ppermute | solution.py:15
  49.4 0.9 copy-start.5
  56.5 103.4 %collective-permute-start.2 = (s32[1024]{0:T(1024)S(1)}, s32[1024]{0:T(1024)S(1)}, u32[]{:S(2)}, u32[]{:S(2)}) collective-permute-start(s32[1024]{0:T(1024)S(1)} %pad_add_fusion), channel_id=1, source_target_pairs={{0,2},{2,4},{4,6},{6,8},{8,10},{10,12},{12,14},{14,16},{16,18},{18... | collective-permute-start | bytes 12296 | tf_op jit(solution)/shard_map/ppermute | solution.py:11
  59.3 110.3 %collective-permute-start.5 = (bf16[64,3584]{1,0:T(8,128)(2,1)S(1)}, bf16[64,3584]{1,0:T(8,128)(2,1)S(1)}, u32[]{:S(2)}, u32[]{:S(2)}) collective-permute-start(bf16[64,3584]{1,0:T(8,128)(2,1)S(1)} %fusion.20), channel_id=1, source_target_pairs={{0,2},{2,4},{4,6},{6,8},{8,10},{10,12},{12,14},{14,16},{16,18},{18... | collective-permute-start | bytes 1376264 | tf_op jit(solution)/shard_map/ppermute | solution.py:11
  60.3 129.0 %collective-permute-start.3 = (bf16[128,3584]{1,0:T(8,128)(2,1)}, bf16[128,3584]{1,0:T(8,128)(2,1)S(1)}, u32[]{:S(2)}, u32[]{:S(2)}) collective-permute-start(bf16[128,3584]{1,0:T(8,128)(2,1)} %fusion.19), channel_id=1, source_target_pairs={{0,2},{2,4},{4,6},{6,8},{8,10},{10,12},{12,14},{14,16},{16,18},{18... | collective-permute-start | bytes 2752520 | tf_op jit(solution)/shard_map/ppermute | solution.py:11
  159.9 4.2 %copy-start.2 = (s32[1024]{0:T(1024)}, s32[1024]{0:T(1024)S(1)}, u32[]{:S(2)}) copy-start(s32[1024]{0:T(1024)S(1)} %collective-permute-done.2) | copy-start | bytes 12292
  193.4 3.5 %slice-start = ((s32[1024]{0:T(1024)}), s32[64]{0:T(128)S(1)}, s32[]{:S(2)}) async-start(s32[1024]{0:T(1024)} %copy-done.2), calls=%async_computation | async-start | bytes 1024 | tf_op jit(solution)/shard_map/slice | solution.py:100

commit v5 on v3

--- a/solution.py
+++ b/solution.py
@@ -3,7 +3,7 @@
 from jax import lax
 from jax.sharding import PartitionSpec as P
 
-LEAD_ROWS = 64
+LEAD_ROWS = 48
 
 
 def passed_along(x, axis, by):
@@ -47,7 +47,7 @@
     hole = kept & (row_iota < bulk)
     free = jnp.logical_not(kept) & (row_iota >= bulk)
     hole_rank, free_rank = earlier(hole, free)
-    n_holes = jnp.sum(hole.astype(jnp.int32))
+    n_holes = hole_rank[bulk]
     used = free & (free_rank < n_holes)
     top_hole, tail_used = hole[:bulk], used[bulk:]
     pairs = top_hole[:, None] & tail_used[None, :] & (hole_rank[:bulk, None] == free_rank[None, bulk:])
@@ -93,17 +93,16 @@
     second = passed_along(second, "section", 1)
     mate = passed_along(mate, "section", 1)
     tail_mate = mate[bulk:]
-    top_mate = jnp.where(row_iota < bulk, mate, -1)
-    back_top = (top_mate[:, None] == tail_iota[None, :]).astype(jnp.bfloat16)
-    out = jnp.where((top_mate >= 0)[:, None],
-                    jnp.dot(back_top, second, preferred_element_type=jnp.float32).astype(jnp.bfloat16),
-                    jnp.concatenate(moved_first + [second], axis=0))
     back_tail = (tail_mate[:, None] == row_iota[None, :bulk]).astype(jnp.bfloat16)
     raw_low = sum(jnp.dot(back_tail[:, a:b], part, preferred_element_type=jnp.float32)
                   for (a, b), part in zip(cuts, moved_first)).astype(jnp.bfloat16)
     raw_low = lax.optimization_barrier(raw_low)
     low = jnp.where((tail_mate >= 0)[:, None], raw_low, second)
-    out = lax.dynamic_update_slice(out, low, (bulk, 0))
+    top_mate = jnp.where(row_iota < bulk, mate, -1)
+    back_top = (top_mate[:, None] == tail_iota[None, :]).astype(jnp.bfloat16)
+    out = jnp.where((top_mate >= 0)[:, None],
+                    jnp.dot(back_top, second, preferred_element_type=jnp.float32).astype(jnp.bfloat16),
+                    jnp.concatenate(moved_first + [low], axis=0))
     return out[None]
 
 

time: 199 us -> 198 us (level)
  transfers between devices with their start and end apart: 6 -> 6, of which waited for: 4 -> 4; matrix products, arithmetic and copies ran while one was open for 22% -> 23% of each run, Pallas kernels for 0% -> 0%
where the time goes in v5:
time: 198 us
  waiting for transfers between devices  124 us (63%)
  matrix products  51.1 us (26%)
  other arithmetic  13.9 us (7%)
  starting transfers between devices  6.46 us (3%)
  local copies, waits for them, and re-layouts  2.03 us (1%)
    ppermute x4, waiting for transfers between devices, passed_along(): lax.ppermute(x, axis, [(i, (i + by) % devices) for i in range(devices)])  123 us
    dot_general x1, matrix products, local(): jnp.dot(back_top, second, preferred_element_type=jnp.float32)  8.59 us
    dot_general x2, matrix products, local(): jnp.dot(pairs[a:b].astype(jnp.bfloat16), current[bulk:], preferred_elemen...  7.19 us
    dot_general x1, matrix products, local(): jnp.dot(normed, table, preferred_element_type=jnp.float32)  6.58 us
    dot_general x1, matrix products, expert_part(): partial_out = jnp.dot(active, down_dev, preferred_element_type=jnp.float32)  6.5 us
    dot_general x1, matrix products, local(): jnp.dot(onehot, normed, preferred_element_type=jnp.float32)  6.47 us
    dot_general x1, matrix products, local(): jnp.dot(carry, new_rows, preferred_element_type=jnp.float32)  6.12 us
    reduce_sum x1, other arithmetic, local(): jnp.sum((ids[:, :, None] == expert_iota[None, None, :]).astype(jnp.float3...  5.75 us
  transfers between devices with their start and end apart: 6, of which 4 were waited for; matrix products, arithmetic and copies ran while one was open for 23% of the time, Pallas kernels for 0%

profile of v5, /device:TPU:1, one launch (start us, length us, event | category | flops | bytes accessed | tf_op | source)
XLA Modules:
  0.0 198.0 jit_solution(1172480855348691351)
XLA Ops:
  0.0 0.9 convert_reduce_fusion.1
  1.4 4.6 %fusion = f32[1024]{0:T(1024)S(1)} fusion(bf16[1,1024,3584]{2,1,0:T(8,128)(2,1)} %param.7), kind=kLoop, calls=%fused_computation.2 | loop fusion | flops 11009024 | bytes 7344128 | tf_op jit(solution)/shard_map/reduce_sum | solution.py:67
  6.0 6.5 %fusion.17 = bf16[128,3584]{1,0:T(8,128)(2,1)} fusion(bf16[1,1024,3584]{2,1,0:T(8,128)(2,1)} %param.7, f32[3584]{0:T(1024)S(1)} %reduce.2, f32[1024]{0:T(1024)S(1)} %add_rsqrt_fusion, s32[1024]{0:T(1024)S(1)} %convert_element_type.77, pred[1024]{0:T(1024)(128)(4,1)S(1)} %get-tuple-element.16), kind=kOutput, calls=%fused_computation.25 | convolution fusion | flops 954925056 | bytes 8281088 | tf_op jit(solution)/shard_map/dot_general | solution.py:75
  12.5 1.4 collective-permute-start
  15.7 0.7 select_reduce_fusion.1
  16.4 5.7 %bitcast_select_fusion = bf16[848,3584]{1,0:T(8,128)(2,1)} fusion(bf16[1,1024,3584]{2,1,0:T(8,128)(2,1)} %param.7, pred[848]{0:T(1024)(128)(4,1)S(1)} %slice.121, pred[896,128]{1,0:T(8,128)(4,1)S(1)} %get-tuple-element.14), kind=kOutput, calls=%fused_computation.20 | convolution fusion | flops 784121856 | bytes 13184000 | tf_op jit(solution)/shard_map/dot_general | solution.py:60
  22.1 1.3 collective-permute-start.5
  23.6 5.7 %convert_reduce_fusion = f32[1024,128]{1,0:T(8,128)S(1)} fusion(s32[1024,8]{1,0:T(8,128)S(1)} %copy.10), kind=kLoop, calls=%fused_computation.29 | loop fusion | flops 3014656 | bytes 557056 | tf_op jit(solution)/shard_map/reduce_sum | solution.py:71
  29.6 6.6 %multiply_reduce_fusion = (f32[1024]{0:T(1024)S(1)}, f32[1024,128]{0,1:T(8,128)}) fusion(f32[1024,128]{0,1:T(8,128)S(1)} %copy.11, bf16[1,3584,128]{2,1,0:T(8,128)(2,1)S(1)} %copy-done, bf16[1,1024,3584]{2,1,0:T(8,128)(2,1)} %param.7, f32[3584]{0:T(1024)S(1)} %reduce.2, f32[1024]{0:T(1024)S(1)} %add_rsqrt_fusion), kind=kOutput, calls=%fused_computation.60 | convolution fusion | flops 954858496 | bytes 9328640 | tf_op jit(solution)/shard_map/dot_general | solution.py:69
  36.2 4.1 %fusion.27 = f32[256,512]{1,0:T(8,128)} fusion(bf16[1,3584,512]{2,1,0:T(8,128)(2,1)S(1)} %copy-done.3, bf16[128,3584]{1,0:T(8,128)(2,1)} %collective-permute-done, bf16[128,3584]{1,0:T(8,128)(2,1)} %fusion.17, pred[]{:T(512)S(6)} %eq.106), kind=kOutput, calls=%fused_computation.37 | convolution fusion | flops 947781632 | bytes 6029313 | tf_op jit(solution)/shard_map/dot_general | solution.py:19
  40.3 6.5 %convolution_convert_fusion.2 = bf16[256,3584]{1,0:T(8,128)(2,1)S(1)} fusion(bf16[1,512,3584]{2,1,0:T(8,128)(2,1)} %param.12, f32[256,512]{1,0:T(8,128)} %fusion.27, bf16[1,3584,512]{2,1,0:T(8,128)(2,1)} %param.11, bf16[128,3584]{1,0:T(8,128)(2,1)} %collective-permute-done, bf16[128,3584]{1,0:T(8,128)(2,1)} %fusion.17, pred[]{:T(512)S(6)} %eq.106), kind=kOutput, calls=%fused_computation.21 | convolution fusion | flops 1889009664 | bytes 11534337 | tf_op jit(solution)/shard_map/dot_general | solution.py:22
  47.3 0.8 slice_multiply_fusion
  48.5 1.0 collective-permute-done.1
  49.5 1.0 copy-done.4
  50.4 6.1 %fusion.20 = bf16[128,3584]{1,0:T(8,128)(2,1)} fusion(bf16[128,3584]{1,0:T(8,128)(2,1)} %copy-done.4, f32[128]{0:T(128)S(1)} %convolution_bitcast_fusion, pred[128]{0:T(512)(128)(4,1)S(1)} %get-tuple-element.12, pred[]{:T(512)S(6)} %eq.106, bf16[1,1024,3584]{2,1,0:T(8,128)(2,1)} %param.7, bf16[256,3584]{1,0:T(8,128)(2,1)S(1)} %convolution_convert_fusion.2, ...), kind=kOutput, calls=%fused_computation.26 | convolution fusion | flops 1061371904 | bytes 11933825 | tf_op jit(solution)/shard_map/dot_general | solution.py:90
  56.6 1.2 collective-permute-start.2
  57.8 1.5 fusion.21
  59.3 1.0 collective-permute-start.4
  60.3 1.2 collective-permute-start.3
  61.5 100.9 %collective-permute-done.2 = s32[1024]{0:T(1024)S(1)} collective-permute-done((s32[1024]{0:T(1024)S(1)}, s32[1024]{0:T(1024)S(1)}, u32[]{:S(2)}, u32[]{:S(2)}) %collective-permute-start.2) | collective-permute-done | bytes 4128 | tf_op jit(solution)/shard_map/ppermute | solution.py:11
  162.5 3.9 %fusion.61 = f32[128,3584]{1,0:T(8,128)S(1)} fusion(bf16[848,3584]{1,0:T(8,128)(2,1)} %collective-permute-done.5, pred[128,896]{1,0:T(32,128)(4,1)S(1)} %broadcast_compare_fusion), kind=kOutput, calls=%fused_computation.67 | convolution fusion | flops 778043392 | bytes 8028160 | tf_op jit(solution)/shard_map/dot_general | solution.py:97
  166.4 3.2 %collective-permute-done.4 = bf16[48,3584]{1,0:T(8,128)(2,1)S(1)} collective-permute-done((bf16[48,3584]{1,0:T(8,128)(2,1)S(1)}, bf16[48,3584]{1,0:T(8,128)(2,1)S(1)}, u32[]{:S(2)}, u32[]{:S(2)}) %collective-permute-start.4) | collective-permute-done | bytes 344096 | tf_op jit(solution)/shard_map/ppermute | solution.py:11
  170.0 19.3 %collective-permute-done.3 = bf16[128,3584]{1,0:T(8,128)(2,1)S(1)} collective-permute-done((bf16[128,3584]{1,0:T(8,128)(2,1)}, bf16[128,3584]{1,0:T(8,128)(2,1)S(1)}, u32[]{:S(2)}, u32[]{:S(2)}) %collective-permute-start.3) | collective-permute-done | bytes 917536 | tf_op jit(solution)/shard_map/ppermute | solution.py:11
  189.4 8.6 %fusion.8 = bf16[1,1024,3584]{2,1,0:T(8,128)(2,1)} fusion(bf16[128,3584]{1,0:T(8,128)(2,1)S(1)} %broadcast_select_fusion, bf16[848,3584]{1,0:T(8,128)(2,1)} %collective-permute-done.5, bf16[48,3584]{1,0:T(8,128)(2,1)S(1)} %collective-permute-done.4, pred[1024]{0:T(1024)(128)(4,1)S(1)} %broadcast_compare_fusion.1, ...), kind=kOutput, calls=%fused_computation.11 | convolution fusion | flops 969015296 | bytes 15602688 | tf_op jit(solution)/shard_map/dot_general | solution.py:104
  (48 shorter events, 4.3 us)
Async XLA Ops:
  0.0 29.6 %copy-start = (bf16[1,3584,128]{2,1,0:T(8,128)(2,1)S(1)}, bf16[1,3584,128]{2,1,0:T(8,128)(2,1)}, u32[]{:S(2)}) copy-start(bf16[1,3584,128]{2,1,0:T(8,128)(2,1)} %param.9) | copy-start | bytes 2752516
  1.4 4.6 %copy-start.2 = (f32[1,3584]{1,0:T(1,128)S(1)}, f32[1,3584]{1,0:T(1,128)}, u32[]{:S(2)}) copy-start(f32[1,3584]{1,0:T(1,128)} %param.8) | copy-start | bytes 43012
  12.5 23.7 %collective-permute-start = (bf16[128,3584]{1,0:T(8,128)(2,1)}, bf16[128,3584]{1,0:T(8,128)(2,1)}, u32[]{:S(2)}, u32[]{:S(2)}) collective-permute-start(bf16[128,3584]{1,0:T(8,128)(2,1)} %fusion.17), channel_id=1, source_target_pairs={{0,1},{1,0},{2,3},{3,2},{4,5},{5,4},{6,7},{7,6},{8,9},{9,8},{10,11... | collective-permute-start | bytes 2752520 | tf_op jit(solution)/shard_map/ppermute | solution.py:15
  16.4 7.0 %copy-start.1 = (s32[1,1,1024,8]{2,3,1,0:T(8,128)S(1)}, s32[1,1,1024,8]{2,3,1,0:T(8,128)}, u32[]{:S(2)}) copy-start(s32[1,1,1024,8]{2,3,1,0:T(8,128)} %param.13) | copy-start | bytes 98308
  22.1 140.4 %collective-permute-start.5 = (bf16[848,3584]{1,0:T(8,128)(2,1)}, bf16[848,3584]{1,0:T(8,128)(2,1)}, u32[]{:S(2)}, u32[]{:S(2)}) collective-permute-start(bf16[848,3584]{1,0:T(8,128)(2,1)} %bitcast_select_fusion), channel_id=1, source_target_pairs={{0,2},{2,4},{4,6},{6,8},{8,10},{10,12},{12,14},{14,16},{16,18},{18... | collective-permute-start | bytes 18235400 | tf_op jit(solution)/shard_map/ppermute | solution.py:11
  29.6 6.6 %copy-start.3 = (bf16[1,3584,512]{2,1,0:T(8,128)(2,1)S(1)}, bf16[1,3584,512]{2,1,0:T(8,128)(2,1)}, u32[]{:S(2)}) copy-start(bf16[1,3584,512]{2,1,0:T(8,128)(2,1)} %param.10) | copy-start | bytes 11010052
  46.9 2.6 %collective-permute-start.1 = (bf16[128,3584]{1,0:T(8,128)(2,1)S(1)}, bf16[128,3584]{1,0:T(8,128)(2,1)S(1)}, u32[]{:S(2)}, u32[]{:S(2)}) collective-permute-start(bf16[128,3584]{1,0:T(8,128)(2,1)S(1)} %broadcast_select_fusion.1), channel_id=1, source_target_pairs={{0,1},{1,0},{2,3},{3,2},{4,5},{5,4},{6,7},{7,6},{8,9},{9,8},{10,11... | collective-permute-start | bytes 2752520 | tf_op jit(solution)/shard_map/ppermute | solution.py:15
  49.5 1.0 copy-start.4
  56.6 105.8 %collective-permute-start.2 = (s32[1024]{0:T(1024)S(1)}, s32[1024]{0:T(1024)S(1)}, u32[]{:S(2)}, u32[]{:S(2)}) collective-permute-start(s32[1024]{0:T(1024)S(1)} %pad_add_fusion), channel_id=1, source_target_pairs={{0,2},{2,4},{4,6},{6,8},{8,10},{10,12},{12,14},{14,16},{16,18},{18... | collective-permute-start | bytes 12296 | tf_op jit(solution)/shard_map/ppermute | solution.py:11
  59.3 110.3 %collective-permute-start.4 = (bf16[48,3584]{1,0:T(8,128)(2,1)S(1)}, bf16[48,3584]{1,0:T(8,128)(2,1)S(1)}, u32[]{:S(2)}, u32[]{:S(2)}) collective-permute-start(bf16[48,3584]{1,0:T(8,128)(2,1)S(1)} %fusion.21), channel_id=1, source_target_pairs={{0,2},{2,4},{4,6},{6,8},{8,10},{10,12},{12,14},{14,16},{16,18},{18... | collective-permute-start | bytes 1032200 | tf_op jit(solution)/shard_map/ppermute | solution.py:11
  60.3 129.0 %collective-permute-start.3 = (bf16[128,3584]{1,0:T(8,128)(2,1)}, bf16[128,3584]{1,0:T(8,128)(2,1)S(1)}, u32[]{:S(2)}, u32[]{:S(2)}) collective-permute-start(bf16[128,3584]{1,0:T(8,128)(2,1)} %fusion.20), channel_id=1, source_target_pairs={{0,2},{2,4},{4,6},{6,8},{8,10},{10,12},{12,14},{14,16},{16,18},{18... | collective-permute-start | bytes 2752520 | tf_op jit(solution)/shard_map/ppermute | solution.py:11
